TPU v7x, 32 devices: a whole 2x2x4 slice. The times are simulated.
32 devices in a mesh: gx: 16 (over z, y, x), gy: 2 (over core).
Axes of the slice: x: 2, y: 2, z: 4, core: 2. Of those that a mesh axis runs over, the one named last changes fastest.
Arguments:
- load_parts: bfloat16 [16, 2, 4, 192, 384], P('gx', 'gy'), may hold values from -6 to 6
- schur: bfloat16 [16, 2, 4, 384, 384], P('gx', 'gy'), may hold values from -4 to 4
- deluxe: bfloat16 [16, 2, 4, 384, 384], P('gx', 'gy'), may hold values from -4 to 4
- panels: bfloat16 [16, 2, 4, 384, 384], P('gx', 'gy'), may hold values from -4 to 4
- coarse_inverse: float32 [128, 128], P(('gx', 'gy')), may hold values from -1 to 1
- primal_dofs: int32 [16, 2, 4], P('gx', 'gy'), may hold values from 0 to 1535
- damage_flags: int32 [16, 2, 4], P('gx', 'gy'), may hold values 0 or 1
Outputs:
- increment: bfloat16 [16, 2, 4, 192, 384], P('gx', 'gy')
Inputs may be any that keep to these rules, and one draw needn't show every extreme that they name: `primal_dofs`: each entry names a face times 384 plus a position on that face.
All inputs are finite; a program needn't handle non-finite values. No bound on the sum of `damage_flags` on one device may be relied on, other than what follows from the above.
Results may differ from a plain program's by a relative error of at most 0.003.
The roundings to bfloat16 on the way count: a program that leaves them out, or rounds other values in their place, can miss the bound.
Values may be sent and summed in bfloat16 or wider, within the bound.
No kernel may reach another device: no remote copies, remote signals or barrier semaphores. Data moves between devices by JAX's collectives and lax.ppermute only.
A program may use at most 64 MiB of HBM per device.

v0:
```python
import jax
import jax.numpy as jnp
from jax import lax
from jax.sharding import PartitionSpec as P


def with_halo(block, sides, width):
    for axis, dim in sides:
        count = lax.axis_size(axis)
        forward = [(i, i + 1) for i in range(count - 1)]
        backward = [(target, source) for source, target in forward]
        low = lax.ppermute(
            lax.slice_in_dim(block, block.shape[dim] - width, None, axis=dim), axis, forward
        )
        high = lax.ppermute(lax.slice_in_dim(block, 0, width, axis=dim), axis, backward)
        block = jnp.concatenate([low, block, high], axis=dim)
    return block


def face_mul(vectors, matrices):
    return jnp.einsum("fry,fyx->frx", vectors, matrices, preferred_element_type=jnp.float32)


def face_mul_turned(vectors, matrices):
    return jnp.einsum("fry,fxy->frx", vectors, matrices, preferred_element_type=jnp.float32)


def face_pairs(values):
    along_first = with_halo(values[0:2], (("gx", 0),), 1)
    along_second = with_halo(values[2:4], (("gy", 0),), 1)
    return jnp.stack([along_first[0], along_first[3], along_second[0], along_second[3]], axis=0)


def image_pairs(values):
    along_first = with_halo(values[0:2], (("gx", 0),), 1)
    along_second = with_halo(values[2:4], (("gy", 0),), 1)
    return jnp.stack([along_first[0], along_first[3], along_second[0], along_second[3]], axis=0)


def per_device(load_parts, schur, deluxe, panels, coarse_inverse, primal_dofs, damage_flags):
    loads_here = load_parts[0, 0]
    schur_panel = schur[0, 0]
    deluxe_panel = deluxe[0, 0]
    inverse_panel = panels[0, 0]
    primal_slots = primal_dofs[0, 0]
    flag_values = damage_flags[0, 0]
    width = loads_here.shape[2]
    primal_count = primal_slots.shape[0]
    positions = jnp.arange(4 * width, dtype=jnp.int32)
    picks = (primal_slots[:, None] == positions[None, :]).reshape(primal_count, 4, width)
    picks_half = picks.astype(jnp.bfloat16)
    picks_full = picks.astype(jnp.float32)
    flags_full = flag_values.astype(jnp.float32)

    def add_coarse(piece):
        return jnp.dot(coarse_inverse, piece.astype(jnp.float32), precision=lax.Precision.HIGHEST)

    def precondition(resid):
        scaled = face_mul_turned(resid.astype(jnp.bfloat16), deluxe_panel).astype(jnp.bfloat16)
        local_part = face_mul(scaled, inverse_panel)
        extra = face_mul(local_part.astype(jnp.bfloat16), inverse_panel)
        softened = local_part + 0.5 * flags_full[:, None, None] * extra
        primal = jnp.einsum(
            "kfx,frx->kr", picks_half, scaled, preferred_element_type=jnp.float32
        ).astype(jnp.bfloat16)
        coarse = add_coarse(lax.all_gather(primal, ("gx", "gy"), axis=0, tiled=True))
        placed = jnp.einsum("kfx,kr->frx", picks_full, coarse, precision=lax.Precision.HIGHEST)
        weighted = (softened + placed).astype(jnp.bfloat16)
        spread = face_mul(weighted, deluxe_panel).astype(jnp.bfloat16)
        return spread.astype(jnp.float32) + face_pairs(spread).astype(jnp.float32)

    def apply_operator(field):
        bent = face_mul(field.astype(jnp.bfloat16), schur_panel).astype(jnp.bfloat16)
        return bent.astype(jnp.float32) + image_pairs(bent).astype(jnp.float32)

    resid0 = loads_here.astype(jnp.float32) + face_pairs(loads_here).astype(jnp.float32)
    first = precondition(resid0)
    resid1 = resid0 - apply_operator(first)
    second = precondition(resid1)
    top = lax.psum(jnp.sum(resid1 * second, axis=(0, 2)), ("gx", "gy"))
    curved = apply_operator(second)
    bottom = lax.psum(jnp.sum(second * curved, axis=(0, 2)), ("gx", "gy"))
    step_len = top / bottom
    result = (first + step_len[:, None] * second).astype(jnp.bfloat16)
    return result[None, None]


def solution(mesh):
    return jax.shard_map(
        per_device,
        mesh=mesh,
        in_specs=(
            P("gx", "gy", None, None, None),
            P("gx", "gy", None, None, None),
            P("gx", "gy", None, None, None),
            P("gx", "gy", None, None, None),
            P(("gx", "gy"), None),
            P("gx", "gy", None),
            P("gx", "gy", None),
        ),
        out_specs=P("gx", "gy", None, None, None),
        check_vma=False,
    )
```

profile of v0, /device:TPU:10, one launch (start us, length us, event | category | flops | bytes accessed | tf_op | source)
XLA Modules:
  0.0 210.2 jit_solution(9755467577524988544)
XLA Ops:
  0.0 1.3 slice_bitcast_fusion.3
  1.3 3.4 %collective-permute-start = (bf16[1,192,384]{2,1,0:T(8,128)(2,1)S(1)}, bf16[1,192,384]{2,1,0:T(8,128)(2,1)S(1)}, u32[]{:S(2)}, u32[]{:S(2)}) collective-permute-start(bf16[1,192,384]{2,1,0:T(8,128)(2,1)S(1)} %get-tuple-element.23), channel_id=1, source_target_pairs={{0,2},{2,4},{4,6},{6,8},{8,10},{10,12},{12,14},{14,16},{16,18},{18... | collective-permute-start | bytes 442376 | tf_op jit(solution)/shard_map/ppermute | solution.py:12
  4.7 2.4 %collective-permute-start.1 = (bf16[1,192,384]{2,1,0:T(8,128)(2,1)S(1)}, bf16[1,192,384]{2,1,0:T(8,128)(2,1)S(1)}, u32[]{:S(2)}, u32[]{:S(2)}) collective-permute-start(bf16[1,192,384]{2,1,0:T(8,128)(2,1)S(1)} %get-tuple-element.24), channel_id=1, source_target_pairs={{2,0},{4,2},{6,4},{8,6},{10,8},{12,10},{14,12},{16,14},{18,16},{20... | collective-permute-start | bytes 442376 | tf_op jit(solution)/shard_map/ppermute | solution.py:15
  7.2 1.3 collective-permute-start.3
  8.5 3.0 %collective-permute-start.2 = (bf16[1,192,384]{2,1,0:T(8,128)(2,1)S(1)}, bf16[1,192,384]{2,1,0:T(8,128)(2,1)S(1)}, u32[]{:S(2)}, u32[]{:S(2)}) collective-permute-start(bf16[1,192,384]{2,1,0:T(8,128)(2,1)S(1)} %get-tuple-element.26), channel_id=1, source_target_pairs={{0,1},{2,3},{4,5},{6,7},{8,9},{10,11},{12,13},{14,15},{16,17},{18,... | collective-permute-start | bytes 442376 | tf_op jit(solution)/shard_map/ppermute | solution.py:12
  11.6 0.6 multiply_bitcast_fusion
  12.1 0.0 collective-permute-done
  12.2 0.8 collective-permute-done.1
  12.9 0.0 collective-permute-done.3
  12.9 0.0 collective-permute-done.2
  13.0 0.0 copy-start.1
  13.0 0.6 convolution_convert_fusion.5
  13.6 0.0 copy-done.17
  13.7 0.0 copy-done.20
  13.7 0.3 fusion.25
  14.0 34.1 %all-gather = bf16[32,4,192]{2,1,0:T(4,128)(2,1)} all-gather(bf16[1,4,192]{2,1,0:T(4,128)(2,1)S(1)} %fusion.25), channel_id=1, replica_groups=mesh['gx'=16,'gy'=2] {'gx','gy'}, dimensions={0}, use_global_device_ids=true | all-gather | bytes 50688 | tf_op jit(solution)/shard_map/all_gather | solution.py:66
  48.0 1.5 reshape.37
  49.6 1.5 fusion.14
  51.1 0.1 convolution_bitcast_fusion.5
  51.2 1.8 convolution_bitcast_fusion.1
  53.0 2.9 %convolution_convert_fusion.4 = bf16[4,192,384]{2,1,0:T(8,128)(2,1)S(1)} fusion(f32[4,192,384]{2,1,0:T(8,128)} %convolution_bitcast_fusion.1, f32[4,192,384]{2,1,0:T(8,128)} %fusion.14, bf16[1,1,4,384,384]{4,3,2,1,0:T(8,128)(2,1)S(1)} %copy-done.1, bf16[1,1,4,384,384]{4,3,2,1,0:T(8,128)(2,1)S(1)} %copy-done, f32[4]{0:T(128)} %multiply_bitcast_fusion), kind=kOutput, calls=%fused_computation.14 | convolution fusion | flops 454754304 | bytes 5308432 | tf_op jit(solution)/shard_map/fry,fyx->frx/dot_general | solution.py:21
  55.9 0.0 copy-start.41
  55.9 0.1 fusion.56
  56.0 3.5 %collective-permute-start.4 = (bf16[1,192,384]{2,1,0:T(8,128)(2,1)S(1)}, bf16[1,192,384]{2,1,0:T(8,128)(2,1)S(1)}, u32[]{:S(2)}, u32[]{:S(2)}) collective-permute-start(bf16[1,192,384]{2,1,0:T(8,128)(2,1)S(1)} %get-tuple-element.19), channel_id=1, source_target_pairs={{0,2},{2,4},{4,6},{6,8},{8,10},{10,12},{12,14},{14,16},{16,18},{18... | collective-permute-start | bytes 442376 | tf_op jit(solution)/shard_map/ppermute | solution.py:12
  59.5 1.3 collective-permute-start.7
  60.8 3.0 %collective-permute-start.6 = (bf16[1,192,384]{2,1,0:T(8,128)(2,1)S(1)}, bf16[1,192,384]{2,1,0:T(8,128)(2,1)S(1)}, u32[]{:S(2)}, u32[]{:S(2)}) collective-permute-start(bf16[1,192,384]{2,1,0:T(8,128)(2,1)S(1)} %get-tuple-element.21), channel_id=1, source_target_pairs={{0,1},{2,3},{4,5},{6,7},{8,9},{10,11},{12,13},{14,15},{16,17},{18,... | collective-permute-start | bytes 442376 | tf_op jit(solution)/shard_map/ppermute | solution.py:12
  63.9 4.6 %collective-permute-start.5 = (bf16[1,192,384]{2,1,0:T(8,128)(2,1)S(1)}, bf16[1,192,384]{2,1,0:T(8,128)(2,1)S(1)}, u32[]{:S(2)}, u32[]{:S(2)}) collective-permute-start(bf16[1,192,384]{2,1,0:T(8,128)(2,1)S(1)} %get-tuple-element.22), channel_id=1, source_target_pairs={{2,0},{4,2},{6,4},{8,6},{10,8},{12,10},{14,12},{16,14},{18,16},{20... | collective-permute-start | bytes 442376 | tf_op jit(solution)/shard_map/ppermute | solution.py:15
  68.5 0.0 collective-permute-done.4
  68.6 3.3 %collective-permute-done.5 = bf16[1,192,384]{2,1,0:T(8,128)(2,1)S(1)} collective-permute-done((bf16[1,192,384]{2,1,0:T(8,128)(2,1)S(1)}, bf16[1,192,384]{2,1,0:T(8,128)(2,1)S(1)}, u32[]{:S(2)}, u32[]{:S(2)}) %collective-permute-start.5) | collective-permute-done | bytes 147488 | tf_op jit(solution)/shard_map/ppermute | solution.py:15
  71.8 0.5 convolution_convert_fusion.3
  72.4 0.1 copy-done.29
  72.5 0.1 fusion.55
  72.6 3.5 %collective-permute-start.8 = (bf16[1,192,384]{2,1,0:T(8,128)(2,1)S(1)}, bf16[1,192,384]{2,1,0:T(8,128)(2,1)S(1)}, u32[]{:S(2)}, u32[]{:S(2)}) collective-permute-start(bf16[1,192,384]{2,1,0:T(8,128)(2,1)S(1)} %get-tuple-element.15), channel_id=1, source_target_pairs={{0,2},{2,4},{4,6},{6,8},{8,10},{10,12},{12,14},{14,16},{16,18},{18... | collective-permute-start | bytes 442376 | tf_op jit(solution)/shard_map/ppermute | solution.py:12
  76.1 1.3 collective-permute-start.11
  77.4 3.0 %collective-permute-start.10 = (bf16[1,192,384]{2,1,0:T(8,128)(2,1)S(1)}, bf16[1,192,384]{2,1,0:T(8,128)(2,1)S(1)}, u32[]{:S(2)}, u32[]{:S(2)}) collective-permute-start(bf16[1,192,384]{2,1,0:T(8,128)(2,1)S(1)} %get-tuple-element.17), channel_id=1, source_target_pairs={{0,1},{2,3},{4,5},{6,7},{8,9},{10,11},{12,13},{14,15},{16,17},{18,... | collective-permute-start | bytes 442376 | tf_op jit(solution)/shard_map/ppermute | solution.py:12
  80.4 3.6 %collective-permute-start.9 = (bf16[1,192,384]{2,1,0:T(8,128)(2,1)S(1)}, bf16[1,192,384]{2,1,0:T(8,128)(2,1)S(1)}, u32[]{:S(2)}, u32[]{:S(2)}) collective-permute-start(bf16[1,192,384]{2,1,0:T(8,128)(2,1)S(1)} %get-tuple-element.18), channel_id=1, source_target_pairs={{2,0},{4,2},{6,4},{8,6},{10,8},{12,10},{14,12},{16,14},{18,16},{20... | collective-permute-start | bytes 442376 | tf_op jit(solution)/shard_map/ppermute | solution.py:15
  84.1 5.0 %collective-permute-done.9 = bf16[1,192,384]{2,1,0:T(8,128)(2,1)S(1)} collective-permute-done((bf16[1,192,384]{2,1,0:T(8,128)(2,1)S(1)}, bf16[1,192,384]{2,1,0:T(8,128)(2,1)S(1)}, u32[]{:S(2)}, u32[]{:S(2)}) %collective-permute-start.9) | collective-permute-done | bytes 147488 | tf_op jit(solution)/shard_map/ppermute | solution.py:15
  89.2 0.7 convolution_convert_fusion.2
  89.9 0.3 fusion.24
  90.2 1.6 fusion.10
  91.7 35.3 %all-gather.1 = bf16[32,4,192]{2,1,0:T(4,128)(2,1)S(1)} all-gather(bf16[1,4,192]{2,1,0:T(4,128)(2,1)S(1)} %fusion.24), channel_id=1, replica_groups=mesh['gx'=16,'gy'=2] {'gx','gy'}, dimensions={0}, use_global_device_ids=true | all-gather | bytes 50688 | tf_op jit(solution)/shard_map/all_gather | solution.py:66
  127.1 0.1 convolution_bitcast_fusion.4
  127.2 1.8 convolution_bitcast_fusion
  129.0 2.9 %convolution_convert_fusion.1 = bf16[4,192,384]{2,1,0:T(8,128)(2,1)S(1)} fusion(f32[4,192,384]{2,1,0:T(8,128)} %convolution_bitcast_fusion, f32[4,192,384]{2,1,0:T(8,128)} %fusion.10, bf16[1,1,4,384,384]{4,3,2,1,0:T(8,128)(2,1)S(1)} %copy-done.1, bf16[1,1,4,384,384]{4,3,2,1,0:T(8,128)(2,1)S(1)} %copy-done, f32[4]{0:T(128)} %multiply_bitcast_fusion), kind=kOutput, calls=%fused_computation.11 | convolution fusion | flops 454754304 | bytes 5308432 | tf_op jit(solution)/shard_map/fry,fyx->frx/dot_general | solution.py:21
  131.9 0.0 copy-start.42
  131.9 0.1 fusion.54
  132.0 2.1 collective-permute-start.12
  134.1 1.3 collective-permute-start.15
  135.4 3.0 %collective-permute-start.14 = (bf16[1,192,384]{2,1,0:T(8,128)(2,1)S(1)}, bf16[1,192,384]{2,1,0:T(8,128)(2,1)S(1)}, u32[]{:S(2)}, u32[]{:S(2)}) collective-permute-start(bf16[1,192,384]{2,1,0:T(8,128)(2,1)S(1)} %get-tuple-element.13), channel_id=1, source_target_pairs={{0,1},{2,3},{4,5},{6,7},{8,9},{10,11},{12,13},{14,15},{16,17},{18,... | collective-permute-start | bytes 442376 | tf_op jit(solution)/shard_map/ppermute | solution.py:12
  138.4 3.9 %collective-permute-start.13 = (bf16[1,192,384]{2,1,0:T(8,128)(2,1)S(1)}, bf16[1,192,384]{2,1,0:T(8,128)(2,1)S(1)}, u32[]{:S(2)}, u32[]{:S(2)}) collective-permute-start(bf16[1,192,384]{2,1,0:T(8,128)(2,1)S(1)} %get-tuple-element.14), channel_id=1, source_target_pairs={{2,0},{4,2},{6,4},{8,6},{10,8},{12,10},{14,12},{16,14},{18,16},{20... | collective-permute-start | bytes 442376 | tf_op jit(solution)/shard_map/ppermute | solution.py:15
  142.4 3.9 %collective-permute-done.13 = bf16[1,192,384]{2,1,0:T(8,128)(2,1)S(1)} collective-permute-done((bf16[1,192,384]{2,1,0:T(8,128)(2,1)S(1)}, bf16[1,192,384]{2,1,0:T(8,128)(2,1)S(1)}, u32[]{:S(2)}, u32[]{:S(2)}) %collective-permute-start.13) | collective-permute-done | bytes 147488 | tf_op jit(solution)/shard_map/ppermute | solution.py:15
  146.4 0.5 convolution_convert_fusion
  147.0 0.0 copy-start.3
  147.0 0.0 copy-start.5
  147.0 0.1 fusion.53
  147.1 2.9 %collective-permute-start.16 = (bf16[1,192,384]{2,1,0:T(8,128)(2,1)S(1)}, bf16[1,192,384]{2,1,0:T(8,128)(2,1)S(1)}, u32[]{:S(2)}, u32[]{:S(2)}) collective-permute-start(bf16[1,192,384]{2,1,0:T(8,128)(2,1)S(1)} %get-tuple-element.7), channel_id=1, source_target_pairs={{0,2},{2,4},{4,6},{6,8},{8,10},{10,12},{12,14},{14,16},{16,18},{18... | collective-permute-start | bytes 442376 | tf_op jit(solution)/shard_map/ppermute | solution.py:12
  149.9 1.3 collective-permute-start.19
  151.2 3.0 %collective-permute-start.18 = (bf16[1,192,384]{2,1,0:T(8,128)(2,1)S(1)}, bf16[1,192,384]{2,1,0:T(8,128)(2,1)S(1)}, u32[]{:S(2)}, u32[]{:S(2)}) collective-permute-start(bf16[1,192,384]{2,1,0:T(8,128)(2,1)S(1)} %get-tuple-element.9), channel_id=1, source_target_pairs={{0,1},{2,3},{4,5},{6,7},{8,9},{10,11},{12,13},{14,15},{16,17},{18,... | collective-permute-start | bytes 442376 | tf_op jit(solution)/shard_map/ppermute | solution.py:12
  154.3 3.4 %collective-permute-start.17 = (bf16[1,192,384]{2,1,0:T(8,128)(2,1)S(1)}, bf16[1,192,384]{2,1,0:T(8,128)(2,1)S(1)}, u32[]{:S(2)}, u32[]{:S(2)}) collective-permute-start(bf16[1,192,384]{2,1,0:T(8,128)(2,1)S(1)} %get-tuple-element.10), channel_id=1, source_target_pairs={{2,0},{4,2},{6,4},{8,6},{10,8},{12,10},{14,12},{16,14},{18,16},{20... | collective-permute-start | bytes 442376 | tf_op jit(solution)/shard_map/ppermute | solution.py:15
  157.8 0.6 multiply_reduce_fusion.1
  158.4 3.8 %collective-permute-done.17 = bf16[1,192,384]{2,1,0:T(8,128)(2,1)S(1)} collective-permute-done((bf16[1,192,384]{2,1,0:T(8,128)(2,1)S(1)}, bf16[1,192,384]{2,1,0:T(8,128)(2,1)S(1)}, u32[]{:S(2)}, u32[]{:S(2)}) %collective-permute-start.17) | collective-permute-done | bytes 147488 | tf_op jit(solution)/shard_map/ppermute | solution.py:15
  162.2 0.4 multiply_reduce_fusion
  162.6 45.2 %all-reduce = (f32[192]{0:T(256)S(1)}, f32[192]{0:T(256)S(1)}) all-reduce(f32[192]{0:T(256)S(1)} %multiply_reduce_fusion.1, f32[192]{0:T(256)S(1)} %multiply_reduce_fusion), channel_id=1, replica_groups=mesh['gx'=16,'gy'=2] {'gx','gy'}, use_global_device_ids=true, to_apply=%region_1.0 | all-reduce | flops 384 | bytes 3072 | tf_op jit(solution)/shard_map/psum | solution.py:80
  207.9 2.3 %fusion.30 = bf16[1,1,4,192,384]{4,3,2,1,0:T(8,128)(2,1)} fusion(bf16[4,192,384]{2,1,0:T(8,128)(2,1)S(1)} %convolution_convert_fusion.1, bf16[4,192,384]{2,1,0:T(8,128)(2,1)S(1)} %convolution_convert_fusion.4, f32[192]{0:T(256)S(1)} %div.3, bf16[1,192,384]{2,1,0:T(8,128)(2,1)S(1)} %copy-done.26, bf16[1,192,384]{2,1,0:T(8,128)(2,1)S(1)} %copy-done.28, ...), kind=kLoop, calls=%fused_computation.46 | loop fusion | flops 4423680 | bytes 2949888 | tf_op jit(solution)/shard_map/broadcast_in_dim | solution.py:85
  (94 shorter events, 0.2 us)
Async XLA Ops:
  0.0 12.9 %copy-start = (bf16[1,1,4,384,384]{4,3,2,1,0:T(8,128)(2,1)S(1)}, bf16[1,1,4,384,384]{4,3,2,1,0:T(8,128)(2,1)}, u32[]{:S(2)}) copy-start(bf16[1,1,4,384,384]{4,3,2,1,0:T(8,128)(2,1)} %param.9) | copy-start | bytes 3538948
  0.0 13.0 %copy-start.2 = (bf16[1,1,4,192,384]{4,3,2,1,0:T(8,128)(2,1)S(1)}, bf16[1,1,4,192,384]{4,3,2,1,0:T(8,128)(2,1)}, u32[]{:S(2)}) copy-start(bf16[1,1,4,192,384]{4,3,2,1,0:T(8,128)(2,1)} %param.7) | copy-start | bytes 1769476
  0.0 11.5 %copy-start.43 = (s32[1,1,4]{2,1,0:T(1,128)S(1)}, s32[1,1,4]{2,1,0:T(1,128)}, u32[]{:S(2)}) copy-start(s32[1,1,4]{2,1,0:T(1,128)} %param.13) | copy-start | bytes 52
  1.3 10.8 %collective-permute-start = (bf16[1,192,384]{2,1,0:T(8,128)(2,1)S(1)}, bf16[1,192,384]{2,1,0:T(8,128)(2,1)S(1)}, u32[]{:S(2)}, u32[]{:S(2)}) collective-permute-start(bf16[1,192,384]{2,1,0:T(8,128)(2,1)S(1)} %get-tuple-element.23), channel_id=1, source_target_pairs={{0,2},{2,4},{4,6},{6,8},{8,10},{10,12},{12,14},{14,16},{16,18},{18... | collective-permute-start | bytes 442376 | tf_op jit(solution)/shard_map/ppermute | solution.py:12
  4.7 8.2 %collective-permute-start.1 = (bf16[1,192,384]{2,1,0:T(8,128)(2,1)S(1)}, bf16[1,192,384]{2,1,0:T(8,128)(2,1)S(1)}, u32[]{:S(2)}, u32[]{:S(2)}) collective-permute-start(bf16[1,192,384]{2,1,0:T(8,128)(2,1)S(1)} %get-tuple-element.24), channel_id=1, source_target_pairs={{2,0},{4,2},{6,4},{8,6},{10,8},{12,10},{14,12},{16,14},{18,16},{20... | collective-permute-start | bytes 442376 | tf_op jit(solution)/shard_map/ppermute | solution.py:15
  7.2 5.7 %collective-permute-start.3 = (bf16[1,192,384]{2,1,0:T(8,128)(2,1)S(1)}, bf16[1,192,384]{2,1,0:T(8,128)(2,1)S(1)}, u32[]{:S(2)}, u32[]{:S(2)}) collective-permute-start(bf16[1,192,384]{2,1,0:T(8,128)(2,1)S(1)} %get-tuple-element.25), channel_id=1, source_target_pairs={{1,0},{3,2},{5,4},{7,6},{9,8},{11,10},{13,12},{15,14},{17,16},{19,... | collective-permute-start | bytes 442376 | tf_op jit(solution)/shard_map/ppermute | solution.py:15
  8.5 4.5 %collective-permute-start.2 = (bf16[1,192,384]{2,1,0:T(8,128)(2,1)S(1)}, bf16[1,192,384]{2,1,0:T(8,128)(2,1)S(1)}, u32[]{:S(2)}, u32[]{:S(2)}) collective-permute-start(bf16[1,192,384]{2,1,0:T(8,128)(2,1)S(1)} %get-tuple-element.26), channel_id=1, source_target_pairs={{0,1},{2,3},{4,5},{6,7},{8,9},{10,11},{12,13},{14,15},{16,17},{18,... | collective-permute-start | bytes 442376 | tf_op jit(solution)/shard_map/ppermute | solution.py:12
  12.1 1.6 copy-start.40
  12.1 1.5 copy-start.11
  12.9 0.7 copy-start.14
  12.9 0.7 copy-start.17
  13.0 0.7 copy-start.20
  13.0 36.6 %copy-start.1 = (bf16[1,1,4,384,384]{4,3,2,1,0:T(8,128)(2,1)S(1)}, bf16[1,1,4,384,384]{4,3,2,1,0:T(8,128)(2,1)}, u32[]{:S(2)}) copy-start(bf16[1,1,4,384,384]{4,3,2,1,0:T(8,128)(2,1)} %param.10) | copy-start | bytes 3538948
  49.6 1.6 copy-start.10
  49.6 1.6 copy-start.39
  55.9 15.9 %copy-start.41 = (bf16[1,1,4,384,384]{4,3,2,1,0:T(8,128)(2,1)S(1)}, bf16[1,1,4,384,384]{4,3,2,1,0:T(8,128)(2,1)}, u32[]{:S(2)}) copy-start(bf16[1,1,4,384,384]{4,3,2,1,0:T(8,128)(2,1)} %param.8) | copy-start | bytes 3538948
  56.0 12.5 %collective-permute-start.4 = (bf16[1,192,384]{2,1,0:T(8,128)(2,1)S(1)}, bf16[1,192,384]{2,1,0:T(8,128)(2,1)S(1)}, u32[]{:S(2)}, u32[]{:S(2)}) collective-permute-start(bf16[1,192,384]{2,1,0:T(8,128)(2,1)S(1)} %get-tuple-element.19), channel_id=1, source_target_pairs={{0,2},{2,4},{4,6},{6,8},{8,10},{10,12},{12,14},{14,16},{16,18},{18... | collective-permute-start | bytes 442376 | tf_op jit(solution)/shard_map/ppermute | solution.py:12
  59.5 9.0 %collective-permute-start.7 = (bf16[1,192,384]{2,1,0:T(8,128)(2,1)S(1)}, bf16[1,192,384]{2,1,0:T(8,128)(2,1)S(1)}, u32[]{:S(2)}, u32[]{:S(2)}) collective-permute-start(bf16[1,192,384]{2,1,0:T(8,128)(2,1)S(1)} %get-tuple-element.20), channel_id=1, source_target_pairs={{1,0},{3,2},{5,4},{7,6},{9,8},{11,10},{13,12},{15,14},{17,16},{19,... | collective-permute-start | bytes 442376 | tf_op jit(solution)/shard_map/ppermute | solution.py:15
  60.8 7.7 %collective-permute-start.6 = (bf16[1,192,384]{2,1,0:T(8,128)(2,1)S(1)}, bf16[1,192,384]{2,1,0:T(8,128)(2,1)S(1)}, u32[]{:S(2)}, u32[]{:S(2)}) collective-permute-start(bf16[1,192,384]{2,1,0:T(8,128)(2,1)S(1)} %get-tuple-element.21), channel_id=1, source_target_pairs={{0,1},{2,3},{4,5},{6,7},{8,9},{10,11},{12,13},{14,15},{16,17},{18,... | collective-permute-start | bytes 442376 | tf_op jit(solution)/shard_map/ppermute | solution.py:12
  63.9 7.9 %collective-permute-start.5 = (bf16[1,192,384]{2,1,0:T(8,128)(2,1)S(1)}, bf16[1,192,384]{2,1,0:T(8,128)(2,1)S(1)}, u32[]{:S(2)}, u32[]{:S(2)}) collective-permute-start(bf16[1,192,384]{2,1,0:T(8,128)(2,1)S(1)} %get-tuple-element.22), channel_id=1, source_target_pairs={{2,0},{4,2},{6,4},{8,6},{10,8},{12,10},{14,12},{16,14},{18,16},{20... | collective-permute-start | bytes 442376 | tf_op jit(solution)/shard_map/ppermute | solution.py:15
  68.5 3.8 %copy-start.23 = (bf16[1,192,384]{2,1,0:T(8,128)(2,1)}, bf16[1,192,384]{2,1,0:T(8,128)(2,1)S(1)}, u32[]{:S(2)}) copy-start(bf16[1,192,384]{2,1,0:T(8,128)(2,1)S(1)} %collective-permute-done.4) | copy-start | bytes 442372
  68.6 3.8 %copy-start.25 = (bf16[1,192,384]{2,1,0:T(8,128)(2,1)}, bf16[1,192,384]{2,1,0:T(8,128)(2,1)S(1)}, u32[]{:S(2)}) copy-start(bf16[1,192,384]{2,1,0:T(8,128)(2,1)S(1)} %collective-permute-done.7) | copy-start | bytes 442372
  68.6 3.8 %copy-start.27 = (bf16[1,192,384]{2,1,0:T(8,128)(2,1)}, bf16[1,192,384]{2,1,0:T(8,128)(2,1)S(1)}, u32[]{:S(2)}) copy-start(bf16[1,192,384]{2,1,0:T(8,128)(2,1)S(1)} %collective-permute-done.6) | copy-start | bytes 442372
  71.8 0.6 copy-start.29
  72.5 17.4 %copy-start.4 = (bf16[4,192,384]{2,1,0:T(8,128)(2,1)}, bf16[4,192,384]{2,1,0:T(8,128)(2,1)S(1)}, u32[]{:S(2)}) copy-start(bf16[4,192,384]{2,1,0:T(8,128)(2,1)S(1)} %convolution_convert_fusion.3) | copy-start | bytes 1769476
  72.5 16.7 %copy-start.12 = (bf16[1,192,384]{2,1,0:T(8,128)(2,1)S(1)}, bf16[1,192,384]{2,1,0:T(8,128)(2,1)}, u32[]{:S(2)}) copy-start(bf16[1,192,384]{2,1,0:T(8,128)(2,1)} %copy-done.11) | copy-start | bytes 442372
  72.5 16.7 %copy-start.15 = (bf16[1,192,384]{2,1,0:T(8,128)(2,1)S(1)}, bf16[1,192,384]{2,1,0:T(8,128)(2,1)}, u32[]{:S(2)}) copy-start(bf16[1,192,384]{2,1,0:T(8,128)(2,1)} %copy-done.14) | copy-start | bytes 442372
  72.5 16.7 %copy-start.18 = (bf16[1,192,384]{2,1,0:T(8,128)(2,1)S(1)}, bf16[1,192,384]{2,1,0:T(8,128)(2,1)}, u32[]{:S(2)}) copy-start(bf16[1,192,384]{2,1,0:T(8,128)(2,1)} %copy-done.17) | copy-start | bytes 442372
  72.5 16.7 %copy-start.21 = (bf16[1,192,384]{2,1,0:T(8,128)(2,1)S(1)}, bf16[1,192,384]{2,1,0:T(8,128)(2,1)}, u32[]{:S(2)}) copy-start(bf16[1,192,384]{2,1,0:T(8,128)(2,1)} %copy-done.20) | copy-start | bytes 442372
  72.6 11.5 %collective-permute-start.8 = (bf16[1,192,384]{2,1,0:T(8,128)(2,1)S(1)}, bf16[1,192,384]{2,1,0:T(8,128)(2,1)S(1)}, u32[]{:S(2)}, u32[]{:S(2)}) collective-permute-start(bf16[1,192,384]{2,1,0:T(8,128)(2,1)S(1)} %get-tuple-element.15), channel_id=1, source_target_pairs={{0,2},{2,4},{4,6},{6,8},{8,10},{10,12},{12,14},{14,16},{16,18},{18... | collective-permute-start | bytes 442376 | tf_op jit(solution)/shard_map/ppermute | solution.py:12
  76.1 8.0 %collective-permute-start.11 = (bf16[1,192,384]{2,1,0:T(8,128)(2,1)S(1)}, bf16[1,192,384]{2,1,0:T(8,128)(2,1)S(1)}, u32[]{:S(2)}, u32[]{:S(2)}) collective-permute-start(bf16[1,192,384]{2,1,0:T(8,128)(2,1)S(1)} %get-tuple-element.16), channel_id=1, source_target_pairs={{1,0},{3,2},{5,4},{7,6},{9,8},{11,10},{13,12},{15,14},{17,16},{19,... | collective-permute-start | bytes 442376 | tf_op jit(solution)/shard_map/ppermute | solution.py:15
  77.4 6.7 %collective-permute-start.10 = (bf16[1,192,384]{2,1,0:T(8,128)(2,1)S(1)}, bf16[1,192,384]{2,1,0:T(8,128)(2,1)S(1)}, u32[]{:S(2)}, u32[]{:S(2)}) collective-permute-start(bf16[1,192,384]{2,1,0:T(8,128)(2,1)S(1)} %get-tuple-element.17), channel_id=1, source_target_pairs={{0,1},{2,3},{4,5},{6,7},{8,9},{10,11},{12,13},{14,15},{16,17},{18,... | collective-permute-start | bytes 442376 | tf_op jit(solution)/shard_map/ppermute | solution.py:12
  80.4 8.7 %collective-permute-start.9 = (bf16[1,192,384]{2,1,0:T(8,128)(2,1)S(1)}, bf16[1,192,384]{2,1,0:T(8,128)(2,1)S(1)}, u32[]{:S(2)}, u32[]{:S(2)}) collective-permute-start(bf16[1,192,384]{2,1,0:T(8,128)(2,1)S(1)} %get-tuple-element.18), channel_id=1, source_target_pairs={{2,0},{4,2},{6,4},{8,6},{10,8},{12,10},{14,12},{16,14},{18,16},{20... | collective-permute-start | bytes 442376 | tf_op jit(solution)/shard_map/ppermute | solution.py:15
  84.1 5.8 %copy-start.31 = (bf16[1,192,384]{2,1,0:T(8,128)(2,1)}, bf16[1,192,384]{2,1,0:T(8,128)(2,1)S(1)}, u32[]{:S(2)}) copy-start(bf16[1,192,384]{2,1,0:T(8,128)(2,1)S(1)} %collective-permute-done.8) | copy-start | bytes 442372
  84.1 5.8 %copy-start.33 = (bf16[1,192,384]{2,1,0:T(8,128)(2,1)}, bf16[1,192,384]{2,1,0:T(8,128)(2,1)S(1)}, u32[]{:S(2)}) copy-start(bf16[1,192,384]{2,1,0:T(8,128)(2,1)S(1)} %collective-permute-done.11) | copy-start | bytes 442372
  84.1 5.8 %copy-start.35 = (bf16[1,192,384]{2,1,0:T(8,128)(2,1)}, bf16[1,192,384]{2,1,0:T(8,128)(2,1)S(1)}, u32[]{:S(2)}) copy-start(bf16[1,192,384]{2,1,0:T(8,128)(2,1)S(1)} %collective-permute-done.10) | copy-start | bytes 442372
  89.2 0.7 copy-start.37
  131.9 14.4 %copy-start.42 = (bf16[1,1,4,384,384]{4,3,2,1,0:T(8,128)(2,1)S(1)}, bf16[1,1,4,384,384]{4,3,2,1,0:T(8,128)(2,1)}, u32[]{:S(2)}) copy-start(bf16[1,1,4,384,384]{4,3,2,1,0:T(8,128)(2,1)} %param.8) | copy-start | bytes 3538948
  132.0 10.3 %collective-permute-start.12 = (bf16[1,192,384]{2,1,0:T(8,128)(2,1)S(1)}, bf16[1,192,384]{2,1,0:T(8,128)(2,1)S(1)}, u32[]{:S(2)}, u32[]{:S(2)}) collective-permute-start(bf16[1,192,384]{2,1,0:T(8,128)(2,1)S(1)} %get-tuple-element.11), channel_id=1, source_target_pairs={{0,2},{2,4},{4,6},{6,8},{8,10},{10,12},{12,14},{14,16},{16,18},{18... | collective-permute-start | bytes 442376 | tf_op jit(solution)/shard_map/ppermute | solution.py:12
  134.1 8.3 %collective-permute-start.15 = (bf16[1,192,384]{2,1,0:T(8,128)(2,1)S(1)}, bf16[1,192,384]{2,1,0:T(8,128)(2,1)S(1)}, u32[]{:S(2)}, u32[]{:S(2)}) collective-permute-start(bf16[1,192,384]{2,1,0:T(8,128)(2,1)S(1)} %get-tuple-element.12), channel_id=1, source_target_pairs={{1,0},{3,2},{5,4},{7,6},{9,8},{11,10},{13,12},{15,14},{17,16},{19,... | collective-permute-start | bytes 442376 | tf_op jit(solution)/shard_map/ppermute | solution.py:15
  135.4 7.0 %collective-permute-start.14 = (bf16[1,192,384]{2,1,0:T(8,128)(2,1)S(1)}, bf16[1,192,384]{2,1,0:T(8,128)(2,1)S(1)}, u32[]{:S(2)}, u32[]{:S(2)}) collective-permute-start(bf16[1,192,384]{2,1,0:T(8,128)(2,1)S(1)} %get-tuple-element.13), channel_id=1, source_target_pairs={{0,1},{2,3},{4,5},{6,7},{8,9},{10,11},{12,13},{14,15},{16,17},{18,... | collective-permute-start | bytes 442376 | tf_op jit(solution)/shard_map/ppermute | solution.py:12
  138.4 7.9 %collective-permute-start.13 = (bf16[1,192,384]{2,1,0:T(8,128)(2,1)S(1)}, bf16[1,192,384]{2,1,0:T(8,128)(2,1)S(1)}, u32[]{:S(2)}, u32[]{:S(2)}) collective-permute-start(bf16[1,192,384]{2,1,0:T(8,128)(2,1)S(1)} %get-tuple-element.14), channel_id=1, source_target_pairs={{2,0},{4,2},{6,4},{8,6},{10,8},{12,10},{14,12},{16,14},{18,16},{20... | collective-permute-start | bytes 442376 | tf_op jit(solution)/shard_map/ppermute | solution.py:15
  142.4 19.9 %copy-start.6 = (bf16[1,192,384]{2,1,0:T(8,128)(2,1)}, bf16[1,192,384]{2,1,0:T(8,128)(2,1)S(1)}, u32[]{:S(2)}) copy-start(bf16[1,192,384]{2,1,0:T(8,128)(2,1)S(1)} %collective-permute-done.12) | copy-start | bytes 442372
  142.4 19.8 %copy-start.7 = (bf16[1,192,384]{2,1,0:T(8,128)(2,1)}, bf16[1,192,384]{2,1,0:T(8,128)(2,1)S(1)}, u32[]{:S(2)}) copy-start(bf16[1,192,384]{2,1,0:T(8,128)(2,1)S(1)} %collective-permute-done.15) | copy-start | bytes 442372
  142.4 19.8 %copy-start.8 = (bf16[1,192,384]{2,1,0:T(8,128)(2,1)}, bf16[1,192,384]{2,1,0:T(8,128)(2,1)S(1)}, u32[]{:S(2)}) copy-start(bf16[1,192,384]{2,1,0:T(8,128)(2,1)S(1)} %collective-permute-done.14) | copy-start | bytes 442372
  146.4 15.9 %copy-start.9 = (bf16[1,192,384]{2,1,0:T(8,128)(2,1)}, bf16[1,192,384]{2,1,0:T(8,128)(2,1)S(1)}, u32[]{:S(2)}) copy-start(bf16[1,192,384]{2,1,0:T(8,128)(2,1)S(1)} %collective-permute-done.13) | copy-start | bytes 442372
  146.4 11.3 %copy-start.13 = (bf16[1,192,384]{2,1,0:T(8,128)(2,1)S(1)}, bf16[1,192,384]{2,1,0:T(8,128)(2,1)}, u32[]{:S(2)}) copy-start(bf16[1,192,384]{2,1,0:T(8,128)(2,1)} %copy-done.11) | copy-start | bytes 442372
  146.4 11.3 %copy-start.16 = (bf16[1,192,384]{2,1,0:T(8,128)(2,1)S(1)}, bf16[1,192,384]{2,1,0:T(8,128)(2,1)}, u32[]{:S(2)}) copy-start(bf16[1,192,384]{2,1,0:T(8,128)(2,1)} %copy-done.14) | copy-start | bytes 442372
  146.4 11.3 %copy-start.19 = (bf16[1,192,384]{2,1,0:T(8,128)(2,1)S(1)}, bf16[1,192,384]{2,1,0:T(8,128)(2,1)}, u32[]{:S(2)}) copy-start(bf16[1,192,384]{2,1,0:T(8,128)(2,1)} %copy-done.17) | copy-start | bytes 442372
  146.4 11.3 %copy-start.22 = (bf16[1,192,384]{2,1,0:T(8,128)(2,1)S(1)}, bf16[1,192,384]{2,1,0:T(8,128)(2,1)}, u32[]{:S(2)}) copy-start(bf16[1,192,384]{2,1,0:T(8,128)(2,1)} %copy-done.20) | copy-start | bytes 442372
  146.4 11.3 %copy-start.32 = (bf16[1,192,384]{2,1,0:T(8,128)(2,1)S(1)}, bf16[1,192,384]{2,1,0:T(8,128)(2,1)}, u32[]{:S(2)}) copy-start(bf16[1,192,384]{2,1,0:T(8,128)(2,1)} %copy-done.31) | copy-start | bytes 442372
  146.4 11.3 %copy-start.34 = (bf16[1,192,384]{2,1,0:T(8,128)(2,1)S(1)}, bf16[1,192,384]{2,1,0:T(8,128)(2,1)}, u32[]{:S(2)}) copy-start(bf16[1,192,384]{2,1,0:T(8,128)(2,1)} %copy-done.33) | copy-start | bytes 442372
  146.4 11.3 %copy-start.36 = (bf16[1,192,384]{2,1,0:T(8,128)(2,1)S(1)}, bf16[1,192,384]{2,1,0:T(8,128)(2,1)}, u32[]{:S(2)}) copy-start(bf16[1,192,384]{2,1,0:T(8,128)(2,1)} %copy-done.35) | copy-start | bytes 442372
  146.4 11.3 %copy-start.38 = (bf16[1,192,384]{2,1,0:T(8,128)(2,1)S(1)}, bf16[1,192,384]{2,1,0:T(8,128)(2,1)}, u32[]{:S(2)}) copy-start(bf16[1,192,384]{2,1,0:T(8,128)(2,1)} %copy-done.37) | copy-start | bytes 442372
  147.0 10.8 %copy-start.3 = (bf16[1,1,4,192,384]{4,3,2,1,0:T(8,128)(2,1)S(1)}, bf16[1,1,4,192,384]{4,3,2,1,0:T(8,128)(2,1)}, u32[]{:S(2)}) copy-start(bf16[1,1,4,192,384]{4,3,2,1,0:T(8,128)(2,1)} %param.7) | copy-start | bytes 1769476
  147.0 10.8 %copy-start.5 = (bf16[4,192,384]{2,1,0:T(8,128)(2,1)S(1)}, bf16[4,192,384]{2,1,0:T(8,128)(2,1)}, u32[]{:S(2)}) copy-start(bf16[4,192,384]{2,1,0:T(8,128)(2,1)} %copy-done.4) | copy-start | bytes 1769476
  147.1 11.3 %collective-permute-start.16 = (bf16[1,192,384]{2,1,0:T(8,128)(2,1)S(1)}, bf16[1,192,384]{2,1,0:T(8,128)(2,1)S(1)}, u32[]{:S(2)}, u32[]{:S(2)}) collective-permute-start(bf16[1,192,384]{2,1,0:T(8,128)(2,1)S(1)} %get-tuple-element.7), channel_id=1, source_target_pairs={{0,2},{2,4},{4,6},{6,8},{8,10},{10,12},{12,14},{14,16},{16,18},{18... | collective-permute-start | bytes 442376 | tf_op jit(solution)/shard_map/ppermute | solution.py:12
  149.9 8.4 %collective-permute-start.19 = (bf16[1,192,384]{2,1,0:T(8,128)(2,1)S(1)}, bf16[1,192,384]{2,1,0:T(8,128)(2,1)S(1)}, u32[]{:S(2)}, u32[]{:S(2)}) collective-permute-start(bf16[1,192,384]{2,1,0:T(8,128)(2,1)S(1)} %get-tuple-element.8), channel_id=1, source_target_pairs={{1,0},{3,2},{5,4},{7,6},{9,8},{11,10},{13,12},{15,14},{17,16},{19,... | collective-permute-start | bytes 442376 | tf_op jit(solution)/shard_map/ppermute | solution.py:15
  151.2 7.1 %collective-permute-start.18 = (bf16[1,192,384]{2,1,0:T(8,128)(2,1)S(1)}, bf16[1,192,384]{2,1,0:T(8,128)(2,1)S(1)}, u32[]{:S(2)}, u32[]{:S(2)}) collective-permute-start(bf16[1,192,384]{2,1,0:T(8,128)(2,1)S(1)} %get-tuple-element.9), channel_id=1, source_target_pairs={{0,1},{2,3},{4,5},{6,7},{8,9},{10,11},{12,13},{14,15},{16,17},{18,... | collective-permute-start | bytes 442376 | tf_op jit(solution)/shard_map/ppermute | solution.py:12
  154.3 7.9 %collective-permute-start.17 = (bf16[1,192,384]{2,1,0:T(8,128)(2,1)S(1)}, bf16[1,192,384]{2,1,0:T(8,128)(2,1)S(1)}, u32[]{:S(2)}, u32[]{:S(2)}) collective-permute-start(bf16[1,192,384]{2,1,0:T(8,128)(2,1)S(1)} %get-tuple-element.10), channel_id=1, source_target_pairs={{2,0},{4,2},{6,4},{8,6},{10,8},{12,10},{14,12},{16,14},{18,16},{20... | collective-permute-start | bytes 442376 | tf_op jit(solution)/shard_map/ppermute | solution.py:15
  158.3 49.5 %copy-start.24 = (bf16[1,192,384]{2,1,0:T(8,128)(2,1)S(1)}, bf16[1,192,384]{2,1,0:T(8,128)(2,1)}, u32[]{:S(2)}) copy-start(bf16[1,192,384]{2,1,0:T(8,128)(2,1)} %copy-done.23) | copy-start | bytes 442372
  158.3 49.5 %copy-start.26 = (bf16[1,192,384]{2,1,0:T(8,128)(2,1)S(1)}, bf16[1,192,384]{2,1,0:T(8,128)(2,1)}, u32[]{:S(2)}) copy-start(bf16[1,192,384]{2,1,0:T(8,128)(2,1)} %copy-done.25) | copy-start | bytes 442372
  158.3 49.5 %copy-start.28 = (bf16[1,192,384]{2,1,0:T(8,128)(2,1)S(1)}, bf16[1,192,384]{2,1,0:T(8,128)(2,1)}, u32[]{:S(2)}) copy-start(bf16[1,192,384]{2,1,0:T(8,128)(2,1)} %copy-done.27) | copy-start | bytes 442372
  158.4 49.5 %copy-start.30 = (bf16[1,192,384]{2,1,0:T(8,128)(2,1)S(1)}, bf16[1,192,384]{2,1,0:T(8,128)(2,1)}, u32[]{:S(2)}) copy-start(bf16[1,192,384]{2,1,0:T(8,128)(2,1)} %copy-done.29) | copy-start | bytes 442372
where the time goes:
time: 211 us; the launch traced here: 210 us
  blocking collectives  115 us (55%)
  starting transfers between devices  55 us (26%)
  waiting for transfers between devices  16.9 us (8%)
  matrix products  15.6 us (7%)
  other arithmetic  3.87 us (2%)
  local copies, waits for them, and re-layouts  3.46 us (2%)
    all_gather x2, blocking collectives, precondition(): lax.all_gather(primal, ('gx', 'gy'), axis=0, tiled=True)  69.4 us
    psum x1, blocking collectives, per_device(): top = lax.psum(jnp.sum(resid1 * second, axis=(0, 2)), ('gx', 'gy'))  45.2 us
    ppermute x10, starting transfers between devices, with_halo(): lax.ppermute(lax.slice_in_dim(block, block.shape[dim] - width, None, axis...  30.5 us
    ppermute x10, starting transfers between devices, with_halo(): lax.ppermute(lax.slice_in_dim(block, 0, width, axis=dim), axis, backward)  24.4 us
    ppermute x10, waiting for transfers between devices, with_halo(): lax.ppermute(lax.slice_in_dim(block, 0, width, axis=dim), axis, backward)  16.8 us
    dot_general x6, matrix products, face_mul(): jnp.einsum('fry,fyx->frx', vectors, matrices, preferred_element_type=jnp....  9.97 us
  transfers between devices with their start and end apart: 20, of which 5 were waited for; matrix products, arithmetic and copies ran while one was open for 1% of the time, Pallas kernels for 0%

commit v1 on v0

--- a/solution.py
+++ b/solution.py
@@ -2,6 +2,18 @@
 import jax.numpy as jnp
 from jax import lax
 from jax.sharding import PartitionSpec as P
+
+
+def collect(x, axis, dim):
+    ways, here, step = (lax.axis_size(axis), lax.axis_index(axis), x.shape[dim])
+    line, have = (x, 1)
+    while have < ways:
+        line = jnp.concatenate(
+            [line, lax.ppermute(line, axis, [(d, (d - have) % ways) for d in range(ways)])],
+            axis=dim,
+        )
+        have = 2 * have
+    return jnp.roll(line, here * step, axis=dim)
 
 
 def with_halo(block, sides, width):
@@ -63,7 +75,7 @@
         primal = jnp.einsum(
             "kfx,frx->kr", picks_half, scaled, preferred_element_type=jnp.float32
         ).astype(jnp.bfloat16)
-        coarse = add_coarse(lax.all_gather(primal, ("gx", "gy"), axis=0, tiled=True))
+        coarse = add_coarse(collect(primal, ("gx", "gy"), 0))
         placed = jnp.einsum("kfx,kr->frx", picks_full, coarse, precision=lax.Precision.HIGHEST)
         weighted = (softened + placed).astype(jnp.bfloat16)
         spread = face_mul(weighted, deluxe_panel).astype(jnp.bfloat16)

time: 211 us -> 194 us (0.919); the launches traced: 210 us -> 191 us
  blocking collectives: 115 us -> 39.6 us
  waiting for transfers between devices: 16.9 us -> 44 us
  starting transfers between devices: 55 us -> 72.9 us
  local copies, waits for them, and re-layouts: 3.46 us -> 10.4 us
  matrix products: 15.6 us -> 18.3 us
    all_gather x2 -> x0, blocking collectives: 69.4 us -> none  [precondition(): lax.all_gather(primal, ('gx', 'gy'), axis=0, tiled=True)]
    ppermute x0 -> x10, starting transfers between devices: none -> 20.9 us  [collect(): lax.ppermute(line, axis, [(d, (d - have) % ways) for d in range(ways)])]
    ppermute x0 -> x10, waiting for transfers between devices: none -> 18.4 us  [collect(): lax.ppermute(line, axis, [(d, (d - have) % ways) for d in range(ways)])]
    ppermute x10, waiting for transfers between devices: 16.8 us -> 25.6 us  [with_halo(): lax.ppermute(lax.slice_in_dim(block, 0, width, axis=dim), axis, backward)]
    concatenate x0 -> x4, local copies, waits for them, and re-layouts: none -> 7.42 us  [collect(): jnp.concatenate([line, lax.ppermute(line, axis, [(d, (d - have) % ways) f...]
    ppermute x10, starting transfers between devices: 24.4 us -> 17.9 us  [with_halo(): lax.ppermute(lax.slice_in_dim(block, 0, width, axis=dim), axis, backward)]
    psum x1, blocking collectives: 45.2 us -> 39.6 us  [per_device(): top = lax.psum(jnp.sum(resid1 * second, axis=(0, 2)), ('gx', 'gy'))]
    ppermute x10, starting transfers between devices: 30.5 us -> 34 us  [with_halo(): lax.ppermute(lax.slice_in_dim(block, block.shape[dim] - width, None, axis...]
  transfers between devices with their start and end apart: 20 -> 30, of which waited for: 5 -> 14; matrix products, arithmetic and copies ran while one was open for 1% -> 3% of each run, Pallas kernels for 0% -> 0%
where the time goes in v1:
time: 194 us; the launch traced here: 191 us
  starting transfers between devices  72.9 us (38%)
  waiting for transfers between devices  44 us (23%)
  blocking collectives  39.6 us (20%)
  matrix products  18.3 us (9%)
  local copies, waits for them, and re-layouts  10.4 us (5%)
  other arithmetic  4.52 us (2%)
    psum x1, blocking collectives, per_device(): top = lax.psum(jnp.sum(resid1 * second, axis=(0, 2)), ('gx', 'gy'))  39.6 us
    ppermute x10, starting transfers between devices, with_halo(): lax.ppermute(lax.slice_in_dim(block, block.shape[dim] - width, None, axis...  34 us
    ppermute x10, waiting for transfers between devices, with_halo(): lax.ppermute(lax.slice_in_dim(block, 0, width, axis=dim), axis, backward)  25.6 us
    ppermute x10, starting transfers between devices, collect(): lax.ppermute(line, axis, [(d, (d - have) % ways) for d in range(ways)])  20.9 us
    ppermute x10, waiting for transfers between devices, collect(): lax.ppermute(line, axis, [(d, (d - have) % ways) for d in range(ways)])  18.4 us
    ppermute x10, starting transfers between devices, with_halo(): lax.ppermute(lax.slice_in_dim(block, 0, width, axis=dim), axis, backward)  17.9 us
    dot_general x6, matrix products, face_mul(): jnp.einsum('fry,fyx->frx', vectors, matrices, preferred_element_type=jnp....  11 us
    concatenate x4, local copies, waits for them, and re-layouts, collect(): jnp.concatenate([line, lax.ppermute(line, axis, [(d, (d - have) % ways) f...  7.42 us
  transfers between devices with their start and end apart: 30, of which 14 were waited for; matrix products, arithmetic and copies ran while one was open for 3% of the time, Pallas kernels for 0%

profile of v1, /device:TPU:10, one launch (start us, length us, event | category | flops | bytes accessed | tf_op | source)
XLA Modules:
  0.0 190.5 jit_solution(9056369682015020239)
XLA Ops:
  0.0 1.3 slice_bitcast_fusion.3
  1.3 3.4 %collective-permute-start = (bf16[1,192,384]{2,1,0:T(8,128)(2,1)S(1)}, bf16[1,192,384]{2,1,0:T(8,128)(2,1)S(1)}, u32[]{:S(2)}, u32[]{:S(2)}) collective-permute-start(bf16[1,192,384]{2,1,0:T(8,128)(2,1)S(1)} %get-tuple-element.24), channel_id=1, source_target_pairs={{0,2},{2,4},{4,6},{6,8},{8,10},{10,12},{12,14},{14,16},{16,18},{18... | collective-permute-start | bytes 442376 | tf_op jit(solution)/shard_map/ppermute | solution.py:24
  4.7 2.4 %collective-permute-start.1 = (bf16[1,192,384]{2,1,0:T(8,128)(2,1)S(1)}, bf16[1,192,384]{2,1,0:T(8,128)(2,1)S(1)}, u32[]{:S(2)}, u32[]{:S(2)}) collective-permute-start(bf16[1,192,384]{2,1,0:T(8,128)(2,1)S(1)} %get-tuple-element.25), channel_id=1, source_target_pairs={{2,0},{4,2},{6,4},{8,6},{10,8},{12,10},{14,12},{16,14},{18,16},{20... | collective-permute-start | bytes 442376 | tf_op jit(solution)/shard_map/ppermute | solution.py:27
  7.2 1.3 collective-permute-start.3
  8.5 3.0 %collective-permute-start.2 = (bf16[1,192,384]{2,1,0:T(8,128)(2,1)S(1)}, bf16[1,192,384]{2,1,0:T(8,128)(2,1)S(1)}, u32[]{:S(2)}, u32[]{:S(2)}) collective-permute-start(bf16[1,192,384]{2,1,0:T(8,128)(2,1)S(1)} %get-tuple-element.27), channel_id=1, source_target_pairs={{0,1},{2,3},{4,5},{6,7},{8,9},{10,11},{12,13},{14,15},{16,17},{18,... | collective-permute-start | bytes 442376 | tf_op jit(solution)/shard_map/ppermute | solution.py:24
  11.6 1.3 collective-permute-done.1
  13.0 0.6 convolution_convert_fusion.5
  14.0 1.8 collective-permute-start.4
  15.8 1.3 collective-permute-done.4
  17.1 0.6 collective-permute-start.5
  17.7 4.0 %collective-permute-done.5 = bf16[8,192]{1,0:T(8,128)(2,1)S(1)} collective-permute-done((bf16[8,192]{1,0:T(8,128)(2,1)S(1)}, bf16[8,192]{1,0:T(8,128)(2,1)S(1)}, u32[]{:S(2)}, u32[]{:S(2)}) %collective-permute-start.5) | collective-permute-done | bytes 3104 | tf_op jit(solution)/shard_map/ppermute | solution.py:12
  21.7 1.5 collective-permute-start.6
  23.1 2.2 %collective-permute-done.6 = bf16[16,192]{1,0:T(8,128)(2,1)S(1)} collective-permute-done((bf16[16,192]{1,0:T(8,128)(2,1)S(1)}, bf16[16,192]{1,0:T(8,128)(2,1)S(1)}, u32[]{:S(2)}, u32[]{:S(2)}) %collective-permute-start.6) | collective-permute-done | bytes 6176 | tf_op jit(solution)/shard_map/ppermute | solution.py:12
  25.4 0.6 copy-done.31
  26.0 0.6 pad_maximum_fusion.5
  26.6 4.5 %collective-permute-start.7 = (bf16[32,192]{1,0:T(8,128)(2,1)}, bf16[32,192]{1,0:T(8,128)(2,1)}, u32[]{:S(2)}, u32[]{:S(2)}) collective-permute-start(bf16[32,192]{1,0:T(8,128)(2,1)} %pad_maximum_fusion.5), channel_id=1, source_target_pairs={{0,24},{1,25},{2,26},{3,27},{4,28},{5,29},{6,30},{7,31},{8,0},{9,1... | collective-permute-start | bytes 36872 | tf_op jit(solution)/shard_map/ppermute | solution.py:12
  31.1 0.6 multiply_bitcast_fusion
  31.7 1.1 collective-permute-done.7
  32.8 4.5 %concatenate.44 = bf16[64,192]{1,0:T(8,128)(2,1)} concatenate(bf16[4,192]{1,0:T(4,128)(2,1)S(1)} %fusion.22, bf16[4,192]{1,0:T(4,128)(2,1)} %copy-done.32, bf16[8,192]{1,0:T(8,128)(2,1)S(1)} %collective-permute-done.5, bf16[16,192]{1,0:T(8,128)(2,1)} %copy-done.31, bf16[32,192]{1,0:T(8,128)(2,1)} %collective-permute-done.7), dimensions={0} | concatenate | bytes 49152 | tf_op jit(solution)/shard_map/concatenate | solution.py:11
  37.3 3.6 %collective-permute-start.8 = (bf16[64,192]{1,0:T(8,128)(2,1)}, bf16[64,192]{1,0:T(8,128)(2,1)}, u32[]{:S(2)}, u32[]{:S(2)}) collective-permute-start(bf16[64,192]{1,0:T(8,128)(2,1)} %concatenate.44), channel_id=1, source_target_pairs={{0,16},{1,17},{2,18},{3,19},{4,20},{5,21},{6,22},{7,23},{8,24},{9,... | collective-permute-start | bytes 73736 | tf_op jit(solution)/shard_map/ppermute | solution.py:12
  40.8 1.6 fusion.14
  42.4 0.6 collective-permute-done.8
  43.1 2.9 %concatenate.45 = bf16[128,192]{1,0:T(8,128)(2,1)S(1)} concatenate(bf16[4,192]{1,0:T(4,128)(2,1)S(1)} %fusion.22, bf16[4,192]{1,0:T(4,128)(2,1)} %copy-done.32, bf16[8,192]{1,0:T(8,128)(2,1)S(1)} %collective-permute-done.5, bf16[16,192]{1,0:T(8,128)(2,1)} %copy-done.31, bf16[32,192]{1,0:T(8,128)(2,1)} %collective-permute-done.7, bf16[64,192]{1,0:T(8,128)(2,1)} %collective-permute-done.8), dimensions={0} | concatenate | bytes 98304 | tf_op jit(solution)/shard_map/concatenate | solution.py:11
  45.9 1.0 convolution_bitcast_fusion.3
  47.0 2.3 %convolution_bitcast_fusion.1 = f32[4,192,384]{2,1,0:T(8,128)} fusion(f32[192,4,1]{1,0,2:T(8,128)S(1)} %convolution_bitcast_fusion.3, s32[4,384]{1,0:T(4,128)S(1)} %multiply_add_fusion, s32[4]{0:T(128)} %bitcast.74), kind=kOutput, calls=%fused_computation.7 | convolution fusion | flops 14161920 | bytes 1188880 | tf_op jit(solution)/shard_map/kfx,kr->frx/dot_general | solution.py:79
  49.3 2.9 %convolution_convert_fusion.4 = bf16[4,192,384]{2,1,0:T(8,128)(2,1)S(1)} fusion(f32[4,192,384]{2,1,0:T(8,128)} %convolution_bitcast_fusion.1, f32[4,192,384]{2,1,0:T(8,128)} %fusion.14, bf16[1,1,4,384,384]{4,3,2,1,0:T(8,128)(2,1)S(1)} %copy-done.1, bf16[1,1,4,384,384]{4,3,2,1,0:T(8,128)(2,1)S(1)} %copy-done, f32[4]{0:T(128)} %multiply_bitcast_fusion), kind=kOutput, calls=%fused_computation.14 | convolution fusion | flops 454754304 | bytes 5308432 | tf_op jit(solution)/shard_map/fry,fyx->frx/dot_general | solution.py:33
  52.3 3.4 %collective-permute-start.9 = (bf16[1,192,384]{2,1,0:T(8,128)(2,1)S(1)}, bf16[1,192,384]{2,1,0:T(8,128)(2,1)S(1)}, u32[]{:S(2)}, u32[]{:S(2)}) collective-permute-start(bf16[1,192,384]{2,1,0:T(8,128)(2,1)S(1)} %get-tuple-element.20), channel_id=1, source_target_pairs={{0,2},{2,4},{4,6},{6,8},{8,10},{10,12},{12,14},{14,16},{16,18},{18... | collective-permute-start | bytes 442376 | tf_op jit(solution)/shard_map/ppermute | solution.py:24
  55.7 1.3 collective-permute-start.12
  57.0 3.0 %collective-permute-start.11 = (bf16[1,192,384]{2,1,0:T(8,128)(2,1)S(1)}, bf16[1,192,384]{2,1,0:T(8,128)(2,1)S(1)}, u32[]{:S(2)}, u32[]{:S(2)}) collective-permute-start(bf16[1,192,384]{2,1,0:T(8,128)(2,1)S(1)} %get-tuple-element.22), channel_id=1, source_target_pairs={{0,1},{2,3},{4,5},{6,7},{8,9},{10,11},{12,13},{14,15},{16,17},{18,... | collective-permute-start | bytes 442376 | tf_op jit(solution)/shard_map/ppermute | solution.py:24
  60.0 2.6 %collective-permute-start.10 = (bf16[1,192,384]{2,1,0:T(8,128)(2,1)S(1)}, bf16[1,192,384]{2,1,0:T(8,128)(2,1)S(1)}, u32[]{:S(2)}, u32[]{:S(2)}) collective-permute-start(bf16[1,192,384]{2,1,0:T(8,128)(2,1)S(1)} %get-tuple-element.23), channel_id=1, source_target_pairs={{2,0},{4,2},{6,4},{8,6},{10,8},{12,10},{14,12},{16,14},{18,16},{20... | collective-permute-start | bytes 442376 | tf_op jit(solution)/shard_map/ppermute | solution.py:27
  62.7 7.7 %collective-permute-done.10 = bf16[1,192,384]{2,1,0:T(8,128)(2,1)S(1)} collective-permute-done((bf16[1,192,384]{2,1,0:T(8,128)(2,1)S(1)}, bf16[1,192,384]{2,1,0:T(8,128)(2,1)S(1)}, u32[]{:S(2)}, u32[]{:S(2)}) %collective-permute-start.10) | collective-permute-done | bytes 147488 | tf_op jit(solution)/shard_map/ppermute | solution.py:27
  70.4 0.5 convolution_convert_fusion.3
  71.2 3.8 %collective-permute-start.13 = (bf16[1,192,384]{2,1,0:T(8,128)(2,1)S(1)}, bf16[1,192,384]{2,1,0:T(8,128)(2,1)S(1)}, u32[]{:S(2)}, u32[]{:S(2)}) collective-permute-start(bf16[1,192,384]{2,1,0:T(8,128)(2,1)S(1)} %get-tuple-element.16), channel_id=1, source_target_pairs={{0,2},{2,4},{4,6},{6,8},{8,10},{10,12},{12,14},{14,16},{16,18},{18... | collective-permute-start | bytes 442376 | tf_op jit(solution)/shard_map/ppermute | solution.py:24
  75.0 1.3 collective-permute-start.16
  76.3 3.0 %collective-permute-start.15 = (bf16[1,192,384]{2,1,0:T(8,128)(2,1)S(1)}, bf16[1,192,384]{2,1,0:T(8,128)(2,1)S(1)}, u32[]{:S(2)}, u32[]{:S(2)}) collective-permute-start(bf16[1,192,384]{2,1,0:T(8,128)(2,1)S(1)} %get-tuple-element.18), channel_id=1, source_target_pairs={{0,1},{2,3},{4,5},{6,7},{8,9},{10,11},{12,13},{14,15},{16,17},{18,... | collective-permute-start | bytes 442376 | tf_op jit(solution)/shard_map/ppermute | solution.py:24
  79.3 2.2 %collective-permute-start.14 = (bf16[1,192,384]{2,1,0:T(8,128)(2,1)S(1)}, bf16[1,192,384]{2,1,0:T(8,128)(2,1)S(1)}, u32[]{:S(2)}, u32[]{:S(2)}) collective-permute-start(bf16[1,192,384]{2,1,0:T(8,128)(2,1)S(1)} %get-tuple-element.19), channel_id=1, source_target_pairs={{2,0},{4,2},{6,4},{8,6},{10,8},{12,10},{14,12},{16,14},{18,16},{20... | collective-permute-start | bytes 442376 | tf_op jit(solution)/shard_map/ppermute | solution.py:27
  81.6 5.7 %collective-permute-done.14 = bf16[1,192,384]{2,1,0:T(8,128)(2,1)S(1)} collective-permute-done((bf16[1,192,384]{2,1,0:T(8,128)(2,1)S(1)}, bf16[1,192,384]{2,1,0:T(8,128)(2,1)S(1)}, u32[]{:S(2)}, u32[]{:S(2)}) %collective-permute-start.14) | collective-permute-done | bytes 147488 | tf_op jit(solution)/shard_map/ppermute | solution.py:27
  87.3 0.6 convolution_convert_fusion.2
  88.3 0.5 copy-done.6
  88.8 1.3 collective-permute-done.17
  90.4 4.4 %collective-permute-done.18 = bf16[8,192]{1,0:T(8,128)(2,1)S(1)} collective-permute-done((bf16[8,192]{1,0:T(8,128)(2,1)S(1)}, bf16[8,192]{1,0:T(8,128)(2,1)S(1)}, u32[]{:S(2)}, u32[]{:S(2)}) %collective-permute-start.18) | collective-permute-done | bytes 3104 | tf_op jit(solution)/shard_map/ppermute | solution.py:12
  94.8 1.8 collective-permute-start.19
  96.5 2.0 %collective-permute-done.19 = bf16[16,192]{1,0:T(8,128)(2,1)S(1)} collective-permute-done((bf16[16,192]{1,0:T(8,128)(2,1)S(1)}, bf16[16,192]{1,0:T(8,128)(2,1)S(1)}, u32[]{:S(2)}, u32[]{:S(2)}) %collective-permute-start.19) | collective-permute-done | bytes 6176 | tf_op jit(solution)/shard_map/ppermute | solution.py:12
  98.6 2.4 %collective-permute-start.20 = (bf16[32,192]{1,0:T(8,128)(2,1)S(1)}, bf16[32,192]{1,0:T(8,128)(2,1)S(1)}, u32[]{:S(2)}, u32[]{:S(2)}) collective-permute-start(bf16[32,192]{1,0:T(8,128)(2,1)S(1)} %pad_maximum_fusion.6), channel_id=1, source_target_pairs={{0,24},{1,25},{2,26},{3,27},{4,28},{5,29},{6,30},{7,31},{8,0},{9,1... | collective-permute-start | bytes 36872 | tf_op jit(solution)/shard_map/ppermute | solution.py:12
  100.9 1.4 collective-permute-done.20
  102.4 4.6 %collective-permute-start.21 = (bf16[64,192]{1,0:T(8,128)(2,1)S(1)}, bf16[64,192]{1,0:T(8,128)(2,1)S(1)}, u32[]{:S(2)}, u32[]{:S(2)}) collective-permute-start(bf16[64,192]{1,0:T(8,128)(2,1)S(1)} %concatenate.49), channel_id=1, source_target_pairs={{0,16},{1,17},{2,18},{3,19},{4,20},{5,21},{6,22},{7,23},{8,24},{9,... | collective-permute-start | bytes 73736 | tf_op jit(solution)/shard_map/ppermute | solution.py:12
  107.0 2.6 %fusion.10 = f32[4,192,384]{2,1,0:T(8,128)} fusion(bf16[4,192,384]{2,1,0:T(8,128)(2,1)} %copy-done.6, bf16[1,1,4,384,384]{4,3,2,1,0:T(8,128)(2,1)S(1)} %copy-done.1), kind=kOutput, calls=%fused_computation.20 | convolution fusion | flops 226492416 | bytes 2949120 | tf_op jit(solution)/shard_map/fry,fyx->frx/dot_general | solution.py:33
  110.0 1.7 convolution_bitcast_fusion
  111.7 2.9 %convolution_convert_fusion.1 = bf16[4,192,384]{2,1,0:T(8,128)(2,1)S(1)} fusion(f32[4,192,384]{2,1,0:T(8,128)} %convolution_bitcast_fusion, f32[4,192,384]{2,1,0:T(8,128)} %fusion.10, bf16[1,1,4,384,384]{4,3,2,1,0:T(8,128)(2,1)S(1)} %copy-done.1, bf16[1,1,4,384,384]{4,3,2,1,0:T(8,128)(2,1)S(1)} %copy-done, f32[4]{0:T(128)S(1)} %copy-done.36), kind=kOutput, calls=%fused_computation.11 | convolution fusion | flops 454754304 | bytes 5308432 | tf_op jit(solution)/shard_map/fry,fyx->frx/dot_general | solution.py:33
  114.7 4.6 %collective-permute-start.22 = (bf16[1,192,384]{2,1,0:T(8,128)(2,1)S(1)}, bf16[1,192,384]{2,1,0:T(8,128)(2,1)S(1)}, u32[]{:S(2)}, u32[]{:S(2)}) collective-permute-start(bf16[1,192,384]{2,1,0:T(8,128)(2,1)S(1)} %get-tuple-element.12), channel_id=1, source_target_pairs={{0,2},{2,4},{4,6},{6,8},{8,10},{10,12},{12,14},{14,16},{16,18},{18... | collective-permute-start | bytes 442376 | tf_op jit(solution)/shard_map/ppermute | solution.py:24
  119.3 1.3 collective-permute-start.25
  120.6 3.0 %collective-permute-start.24 = (bf16[1,192,384]{2,1,0:T(8,128)(2,1)S(1)}, bf16[1,192,384]{2,1,0:T(8,128)(2,1)S(1)}, u32[]{:S(2)}, u32[]{:S(2)}) collective-permute-start(bf16[1,192,384]{2,1,0:T(8,128)(2,1)S(1)} %get-tuple-element.14), channel_id=1, source_target_pairs={{0,1},{2,3},{4,5},{6,7},{8,9},{10,11},{12,13},{14,15},{16,17},{18,... | collective-permute-start | bytes 442376 | tf_op jit(solution)/shard_map/ppermute | solution.py:24
  123.7 1.9 %collective-permute-start.23 = (bf16[1,192,384]{2,1,0:T(8,128)(2,1)S(1)}, bf16[1,192,384]{2,1,0:T(8,128)(2,1)S(1)}, u32[]{:S(2)}, u32[]{:S(2)}) collective-permute-start(bf16[1,192,384]{2,1,0:T(8,128)(2,1)S(1)} %get-tuple-element.15), channel_id=1, source_target_pairs={{2,0},{4,2},{6,4},{8,6},{10,8},{12,10},{14,12},{16,14},{18,16},{20... | collective-permute-start | bytes 442376 | tf_op jit(solution)/shard_map/ppermute | solution.py:27
  125.6 6.0 %collective-permute-done.23 = bf16[1,192,384]{2,1,0:T(8,128)(2,1)S(1)} collective-permute-done((bf16[1,192,384]{2,1,0:T(8,128)(2,1)S(1)}, bf16[1,192,384]{2,1,0:T(8,128)(2,1)S(1)}, u32[]{:S(2)}, u32[]{:S(2)}) %collective-permute-start.23) | collective-permute-done | bytes 147488 | tf_op jit(solution)/shard_map/ppermute | solution.py:27
  131.7 0.5 convolution_convert_fusion
  132.3 3.7 %collective-permute-start.26 = (bf16[1,192,384]{2,1,0:T(8,128)(2,1)S(1)}, bf16[1,192,384]{2,1,0:T(8,128)(2,1)S(1)}, u32[]{:S(2)}, u32[]{:S(2)}) collective-permute-start(bf16[1,192,384]{2,1,0:T(8,128)(2,1)S(1)} %get-tuple-element.8), channel_id=1, source_target_pairs={{0,2},{2,4},{4,6},{6,8},{8,10},{10,12},{12,14},{14,16},{16,18},{18... | collective-permute-start | bytes 442376 | tf_op jit(solution)/shard_map/ppermute | solution.py:24
  136.0 1.3 collective-permute-start.29
  137.3 3.0 %collective-permute-start.28 = (bf16[1,192,384]{2,1,0:T(8,128)(2,1)S(1)}, bf16[1,192,384]{2,1,0:T(8,128)(2,1)S(1)}, u32[]{:S(2)}, u32[]{:S(2)}) collective-permute-start(bf16[1,192,384]{2,1,0:T(8,128)(2,1)S(1)} %get-tuple-element.10), channel_id=1, source_target_pairs={{0,1},{2,3},{4,5},{6,7},{8,9},{10,11},{12,13},{14,15},{16,17},{18,... | collective-permute-start | bytes 442376 | tf_op jit(solution)/shard_map/ppermute | solution.py:24
  140.3 2.3 %collective-permute-start.27 = (bf16[1,192,384]{2,1,0:T(8,128)(2,1)S(1)}, bf16[1,192,384]{2,1,0:T(8,128)(2,1)S(1)}, u32[]{:S(2)}, u32[]{:S(2)}) collective-permute-start(bf16[1,192,384]{2,1,0:T(8,128)(2,1)S(1)} %get-tuple-element.11), channel_id=1, source_target_pairs={{2,0},{4,2},{6,4},{8,6},{10,8},{12,10},{14,12},{16,14},{18,16},{20... | collective-permute-start | bytes 442376 | tf_op jit(solution)/shard_map/ppermute | solution.py:27
  142.7 0.6 multiply_reduce_fusion.1
  143.3 4.9 %collective-permute-done.27 = bf16[1,192,384]{2,1,0:T(8,128)(2,1)S(1)} collective-permute-done((bf16[1,192,384]{2,1,0:T(8,128)(2,1)S(1)}, bf16[1,192,384]{2,1,0:T(8,128)(2,1)S(1)}, u32[]{:S(2)}, u32[]{:S(2)}) %collective-permute-start.27) | collective-permute-done | bytes 147488 | tf_op jit(solution)/shard_map/ppermute | solution.py:27
  148.3 0.4 multiply_reduce_fusion
  148.7 39.6 %all-reduce = (f32[192]{0:T(256)S(1)}, f32[192]{0:T(256)S(1)}) all-reduce(f32[192]{0:T(256)S(1)} %multiply_reduce_fusion.1, f32[192]{0:T(256)S(1)} %multiply_reduce_fusion), channel_id=1, replica_groups=mesh['gx'=16,'gy'=2] {'gx','gy'}, use_global_device_ids=true, to_apply=%region_1.3 | all-reduce | flops 384 | bytes 3072 | tf_op jit(solution)/shard_map/psum | solution.py:92
  188.2 2.3 %fusion.28 = bf16[1,1,4,192,384]{4,3,2,1,0:T(8,128)(2,1)} fusion(bf16[4,192,384]{2,1,0:T(8,128)(2,1)S(1)} %convolution_convert_fusion.1, bf16[4,192,384]{2,1,0:T(8,128)(2,1)S(1)} %convolution_convert_fusion.4, f32[192]{0:T(256)S(1)} %div.3, bf16[1,192,384]{2,1,0:T(8,128)(2,1)} %copy-done.20, bf16[1,192,384]{2,1,0:T(8,128)(2,1)} %copy-done.21, ...), kind=kLoop, calls=%fused_computation.44 | loop fusion | flops 4423680 | bytes 2949888 | tf_op jit(solution)/shard_map/broadcast_in_dim | solution.py:97
  (112 shorter events, 1.9 us)
Async XLA Ops:
  0.0 12.9 %copy-start = (bf16[1,1,4,384,384]{4,3,2,1,0:T(8,128)(2,1)S(1)}, bf16[1,1,4,384,384]{4,3,2,1,0:T(8,128)(2,1)}, u32[]{:S(2)}) copy-start(bf16[1,1,4,384,384]{4,3,2,1,0:T(8,128)(2,1)} %param.11) | copy-start | bytes 3538948
  0.0 12.9 %copy-start.2 = (bf16[1,1,4,192,384]{4,3,2,1,0:T(8,128)(2,1)S(1)}, bf16[1,1,4,192,384]{4,3,2,1,0:T(8,128)(2,1)}, u32[]{:S(2)}) copy-start(bf16[1,1,4,192,384]{4,3,2,1,0:T(8,128)(2,1)} %param.9) | copy-start | bytes 1769476
  1.3 10.2 %collective-permute-start = (bf16[1,192,384]{2,1,0:T(8,128)(2,1)S(1)}, bf16[1,192,384]{2,1,0:T(8,128)(2,1)S(1)}, u32[]{:S(2)}, u32[]{:S(2)}) collective-permute-start(bf16[1,192,384]{2,1,0:T(8,128)(2,1)S(1)} %get-tuple-element.24), channel_id=1, source_target_pairs={{0,2},{2,4},{4,6},{6,8},{8,10},{10,12},{12,14},{14,16},{16,18},{18... | collective-permute-start | bytes 442376 | tf_op jit(solution)/shard_map/ppermute | solution.py:24
  4.7 8.2 %collective-permute-start.1 = (bf16[1,192,384]{2,1,0:T(8,128)(2,1)S(1)}, bf16[1,192,384]{2,1,0:T(8,128)(2,1)S(1)}, u32[]{:S(2)}, u32[]{:S(2)}) collective-permute-start(bf16[1,192,384]{2,1,0:T(8,128)(2,1)S(1)} %get-tuple-element.25), channel_id=1, source_target_pairs={{2,0},{4,2},{6,4},{8,6},{10,8},{12,10},{14,12},{16,14},{18,16},{20... | collective-permute-start | bytes 442376 | tf_op jit(solution)/shard_map/ppermute | solution.py:27
  7.2 5.7 %collective-permute-start.3 = (bf16[1,192,384]{2,1,0:T(8,128)(2,1)S(1)}, bf16[1,192,384]{2,1,0:T(8,128)(2,1)S(1)}, u32[]{:S(2)}, u32[]{:S(2)}) collective-permute-start(bf16[1,192,384]{2,1,0:T(8,128)(2,1)S(1)} %get-tuple-element.26), channel_id=1, source_target_pairs={{1,0},{3,2},{5,4},{7,6},{9,8},{11,10},{13,12},{15,14},{17,16},{19,... | collective-permute-start | bytes 442376 | tf_op jit(solution)/shard_map/ppermute | solution.py:27
  8.5 4.5 %collective-permute-start.2 = (bf16[1,192,384]{2,1,0:T(8,128)(2,1)S(1)}, bf16[1,192,384]{2,1,0:T(8,128)(2,1)S(1)}, u32[]{:S(2)}, u32[]{:S(2)}) collective-permute-start(bf16[1,192,384]{2,1,0:T(8,128)(2,1)S(1)} %get-tuple-element.27), channel_id=1, source_target_pairs={{0,1},{2,3},{4,5},{6,7},{8,9},{10,11},{12,13},{14,15},{16,17},{18,... | collective-permute-start | bytes 442376 | tf_op jit(solution)/shard_map/ppermute | solution.py:24
  11.5 2.1 %copy-start.34 = (s32[1,1,4]{2,1,0:T(1,128)S(1)}, s32[1,1,4]{2,1,0:T(1,128)}, u32[]{:S(2)}) copy-start(s32[1,1,4]{2,1,0:T(1,128)} %param.14) | copy-start | bytes 52
  11.6 19.6 %copy-start.39 = (s32[1,1,4]{2,1,0:T(1,128)S(1)}, s32[1,1,4]{2,1,0:T(1,128)}, u32[]{:S(2)}) copy-start(s32[1,1,4]{2,1,0:T(1,128)} %param.15) | copy-start | bytes 52
  11.6 2.0 %copy-start.7 = (bf16[1,192,384]{2,1,0:T(8,128)(2,1)}, bf16[1,192,384]{2,1,0:T(8,128)(2,1)S(1)}, u32[]{:S(2)}) copy-start(bf16[1,192,384]{2,1,0:T(8,128)(2,1)S(1)} %collective-permute-done) | copy-start | bytes 442372
  13.0 27.9 %copy-start.1 = (bf16[1,1,4,384,384]{4,3,2,1,0:T(8,128)(2,1)S(1)}, bf16[1,1,4,384,384]{4,3,2,1,0:T(8,128)(2,1)}, u32[]{:S(2)}) copy-start(bf16[1,1,4,384,384]{4,3,2,1,0:T(8,128)(2,1)} %param.12) | copy-start | bytes 3538948
  14.0 3.1 %collective-permute-start.4 = (bf16[4,192]{1,0:T(4,128)(2,1)S(1)}, bf16[4,192]{1,0:T(4,128)(2,1)S(1)}, u32[]{:S(2)}, u32[]{:S(2)}) collective-permute-start(bf16[4,192]{1,0:T(4,128)(2,1)S(1)} %fusion.22), channel_id=1, source_target_pairs={{0,31},{1,0},{2,1},{3,2},{4,3},{5,4},{6,5},{7,6},{8,7},{9,8},{10,9... | collective-permute-start | bytes 4616 | tf_op jit(solution)/shard_map/ppermute | solution.py:12
  17.1 9.5 %copy-start.32 = (bf16[4,192]{1,0:T(4,128)(2,1)}, bf16[4,192]{1,0:T(4,128)(2,1)S(1)}, u32[]{:S(2)}) copy-start(bf16[4,192]{1,0:T(4,128)(2,1)S(1)} %collective-permute-done.4) | copy-start | bytes 4612
  17.1 4.6 %collective-permute-start.5 = (bf16[8,192]{1,0:T(8,128)(2,1)S(1)}, bf16[8,192]{1,0:T(8,128)(2,1)S(1)}, u32[]{:S(2)}, u32[]{:S(2)}) collective-permute-start(bf16[8,192]{1,0:T(8,128)(2,1)S(1)} %pad_maximum_fusion.9), channel_id=1, source_target_pairs={{0,30},{1,31},{2,0},{3,1},{4,2},{5,3},{6,4},{7,5},{8,6},{9,7},{10,... | collective-permute-start | bytes 9224 | tf_op jit(solution)/shard_map/ppermute | solution.py:12
  21.7 3.7 %collective-permute-start.6 = (bf16[16,192]{1,0:T(8,128)(2,1)S(1)}, bf16[16,192]{1,0:T(8,128)(2,1)S(1)}, u32[]{:S(2)}, u32[]{:S(2)}) collective-permute-start(bf16[16,192]{1,0:T(8,128)(2,1)S(1)} %pad_maximum_fusion.7), channel_id=1, source_target_pairs={{0,28},{1,29},{2,30},{3,31},{4,0},{5,1},{6,2},{7,3},{8,4},{9,5},{1... | collective-permute-start | bytes 18440 | tf_op jit(solution)/shard_map/ppermute | solution.py:12
  26.6 6.2 %collective-permute-start.7 = (bf16[32,192]{1,0:T(8,128)(2,1)}, bf16[32,192]{1,0:T(8,128)(2,1)}, u32[]{:S(2)}, u32[]{:S(2)}) collective-permute-start(bf16[32,192]{1,0:T(8,128)(2,1)} %pad_maximum_fusion.5), channel_id=1, source_target_pairs={{0,24},{1,25},{2,26},{3,27},{4,28},{5,29},{6,30},{7,31},{8,0},{9,1... | collective-permute-start | bytes 36872 | tf_op jit(solution)/shard_map/ppermute | solution.py:12
  37.3 5.8 %collective-permute-start.8 = (bf16[64,192]{1,0:T(8,128)(2,1)}, bf16[64,192]{1,0:T(8,128)(2,1)}, u32[]{:S(2)}, u32[]{:S(2)}) collective-permute-start(bf16[64,192]{1,0:T(8,128)(2,1)} %concatenate.44), channel_id=1, source_target_pairs={{0,16},{1,17},{2,18},{3,19},{4,20},{5,21},{6,22},{7,23},{8,24},{9,... | collective-permute-start | bytes 73736 | tf_op jit(solution)/shard_map/ppermute | solution.py:12
  52.2 18.2 %copy-start.37 = (bf16[1,1,4,384,384]{4,3,2,1,0:T(8,128)(2,1)S(1)}, bf16[1,1,4,384,384]{4,3,2,1,0:T(8,128)(2,1)}, u32[]{:S(2)}) copy-start(bf16[1,1,4,384,384]{4,3,2,1,0:T(8,128)(2,1)} %param.10) | copy-start | bytes 3538948
  52.3 10.3 %collective-permute-start.9 = (bf16[1,192,384]{2,1,0:T(8,128)(2,1)S(1)}, bf16[1,192,384]{2,1,0:T(8,128)(2,1)S(1)}, u32[]{:S(2)}, u32[]{:S(2)}) collective-permute-start(bf16[1,192,384]{2,1,0:T(8,128)(2,1)S(1)} %get-tuple-element.20), channel_id=1, source_target_pairs={{0,2},{2,4},{4,6},{6,8},{8,10},{10,12},{12,14},{14,16},{16,18},{18... | collective-permute-start | bytes 442376 | tf_op jit(solution)/shard_map/ppermute | solution.py:24
  55.7 7.0 %collective-permute-start.12 = (bf16[1,192,384]{2,1,0:T(8,128)(2,1)S(1)}, bf16[1,192,384]{2,1,0:T(8,128)(2,1)S(1)}, u32[]{:S(2)}, u32[]{:S(2)}) collective-permute-start(bf16[1,192,384]{2,1,0:T(8,128)(2,1)S(1)} %get-tuple-element.21), channel_id=1, source_target_pairs={{1,0},{3,2},{5,4},{7,6},{9,8},{11,10},{13,12},{15,14},{17,16},{19,... | collective-permute-start | bytes 442376 | tf_op jit(solution)/shard_map/ppermute | solution.py:27
  57.0 5.7 %collective-permute-start.11 = (bf16[1,192,384]{2,1,0:T(8,128)(2,1)S(1)}, bf16[1,192,384]{2,1,0:T(8,128)(2,1)S(1)}, u32[]{:S(2)}, u32[]{:S(2)}) collective-permute-start(bf16[1,192,384]{2,1,0:T(8,128)(2,1)S(1)} %get-tuple-element.22), channel_id=1, source_target_pairs={{0,1},{2,3},{4,5},{6,7},{8,9},{10,11},{12,13},{14,15},{16,17},{18,... | collective-permute-start | bytes 442376 | tf_op jit(solution)/shard_map/ppermute | solution.py:24
  60.0 10.4 %collective-permute-start.10 = (bf16[1,192,384]{2,1,0:T(8,128)(2,1)S(1)}, bf16[1,192,384]{2,1,0:T(8,128)(2,1)S(1)}, u32[]{:S(2)}, u32[]{:S(2)}) collective-permute-start(bf16[1,192,384]{2,1,0:T(8,128)(2,1)S(1)} %get-tuple-element.23), channel_id=1, source_target_pairs={{2,0},{4,2},{6,4},{8,6},{10,8},{12,10},{14,12},{16,14},{18,16},{20... | collective-permute-start | bytes 442376 | tf_op jit(solution)/shard_map/ppermute | solution.py:27
  62.7 8.3 %copy-start.19 = (bf16[1,192,384]{2,1,0:T(8,128)(2,1)}, bf16[1,192,384]{2,1,0:T(8,128)(2,1)S(1)}, u32[]{:S(2)}) copy-start(bf16[1,192,384]{2,1,0:T(8,128)(2,1)S(1)} %collective-permute-done.9) | copy-start | bytes 442372
  62.7 8.3 %copy-start.20 = (bf16[1,192,384]{2,1,0:T(8,128)(2,1)}, bf16[1,192,384]{2,1,0:T(8,128)(2,1)S(1)}, u32[]{:S(2)}) copy-start(bf16[1,192,384]{2,1,0:T(8,128)(2,1)S(1)} %collective-permute-done.12) | copy-start | bytes 442372
  62.7 8.3 %copy-start.21 = (bf16[1,192,384]{2,1,0:T(8,128)(2,1)}, bf16[1,192,384]{2,1,0:T(8,128)(2,1)S(1)}, u32[]{:S(2)}) copy-start(bf16[1,192,384]{2,1,0:T(8,128)(2,1)S(1)} %collective-permute-done.11) | copy-start | bytes 442372
  71.1 16.9 %copy-start.4 = (bf16[4,192,384]{2,1,0:T(8,128)(2,1)}, bf16[4,192,384]{2,1,0:T(8,128)(2,1)S(1)}, u32[]{:S(2)}) copy-start(bf16[4,192,384]{2,1,0:T(8,128)(2,1)S(1)} %convolution_convert_fusion.3) | copy-start | bytes 1769476
  71.1 16.2 %copy-start.8 = (bf16[1,192,384]{2,1,0:T(8,128)(2,1)S(1)}, bf16[1,192,384]{2,1,0:T(8,128)(2,1)}, u32[]{:S(2)}) copy-start(bf16[1,192,384]{2,1,0:T(8,128)(2,1)} %copy-done.7) | copy-start | bytes 442372
  71.1 16.2 %copy-start.11 = (bf16[1,192,384]{2,1,0:T(8,128)(2,1)S(1)}, bf16[1,192,384]{2,1,0:T(8,128)(2,1)}, u32[]{:S(2)}) copy-start(bf16[1,192,384]{2,1,0:T(8,128)(2,1)} %copy-done.10) | copy-start | bytes 442372
  71.1 16.2 %copy-start.14 = (bf16[1,192,384]{2,1,0:T(8,128)(2,1)S(1)}, bf16[1,192,384]{2,1,0:T(8,128)(2,1)}, u32[]{:S(2)}) copy-start(bf16[1,192,384]{2,1,0:T(8,128)(2,1)} %copy-done.13) | copy-start | bytes 442372
  71.1 16.2 %copy-start.17 = (bf16[1,192,384]{2,1,0:T(8,128)(2,1)S(1)}, bf16[1,192,384]{2,1,0:T(8,128)(2,1)}, u32[]{:S(2)}) copy-start(bf16[1,192,384]{2,1,0:T(8,128)(2,1)} %copy-done.16) | copy-start | bytes 442372
  71.2 10.4 %collective-permute-start.13 = (bf16[1,192,384]{2,1,0:T(8,128)(2,1)S(1)}, bf16[1,192,384]{2,1,0:T(8,128)(2,1)S(1)}, u32[]{:S(2)}, u32[]{:S(2)}) collective-permute-start(bf16[1,192,384]{2,1,0:T(8,128)(2,1)S(1)} %get-tuple-element.16), channel_id=1, source_target_pairs={{0,2},{2,4},{4,6},{6,8},{8,10},{10,12},{12,14},{14,16},{16,18},{18... | collective-permute-start | bytes 442376 | tf_op jit(solution)/shard_map/ppermute | solution.py:24
  75.0 6.6 %collective-permute-start.16 = (bf16[1,192,384]{2,1,0:T(8,128)(2,1)S(1)}, bf16[1,192,384]{2,1,0:T(8,128)(2,1)S(1)}, u32[]{:S(2)}, u32[]{:S(2)}) collective-permute-start(bf16[1,192,384]{2,1,0:T(8,128)(2,1)S(1)} %get-tuple-element.17), channel_id=1, source_target_pairs={{1,0},{3,2},{5,4},{7,6},{9,8},{11,10},{13,12},{15,14},{17,16},{19,... | collective-permute-start | bytes 442376 | tf_op jit(solution)/shard_map/ppermute | solution.py:27
  76.3 5.3 %collective-permute-start.15 = (bf16[1,192,384]{2,1,0:T(8,128)(2,1)S(1)}, bf16[1,192,384]{2,1,0:T(8,128)(2,1)S(1)}, u32[]{:S(2)}, u32[]{:S(2)}) collective-permute-start(bf16[1,192,384]{2,1,0:T(8,128)(2,1)S(1)} %get-tuple-element.18), channel_id=1, source_target_pairs={{0,1},{2,3},{4,5},{6,7},{8,9},{10,11},{12,13},{14,15},{16,17},{18,... | collective-permute-start | bytes 442376 | tf_op jit(solution)/shard_map/ppermute | solution.py:24
  79.3 8.7 %copy-start.35 = (s32[1,1,4]{2,1,0:T(1,128)S(1)}, s32[1,1,4]{2,1,0:T(1,128)}, u32[]{:S(2)}) copy-start(s32[1,1,4]{2,1,0:T(1,128)} %param.14) | copy-start | bytes 52
  79.3 7.9 %collective-permute-start.14 = (bf16[1,192,384]{2,1,0:T(8,128)(2,1)S(1)}, bf16[1,192,384]{2,1,0:T(8,128)(2,1)S(1)}, u32[]{:S(2)}, u32[]{:S(2)}) collective-permute-start(bf16[1,192,384]{2,1,0:T(8,128)(2,1)S(1)} %get-tuple-element.19), channel_id=1, source_target_pairs={{2,0},{4,2},{6,4},{8,6},{10,8},{12,10},{14,12},{16,14},{18,16},{20... | collective-permute-start | bytes 442376 | tf_op jit(solution)/shard_map/ppermute | solution.py:27
  81.5 6.4 %copy-start.23 = (bf16[1,192,384]{2,1,0:T(8,128)(2,1)}, bf16[1,192,384]{2,1,0:T(8,128)(2,1)S(1)}, u32[]{:S(2)}) copy-start(bf16[1,192,384]{2,1,0:T(8,128)(2,1)S(1)} %collective-permute-done.13) | copy-start | bytes 442372
  81.6 6.4 %copy-start.25 = (bf16[1,192,384]{2,1,0:T(8,128)(2,1)}, bf16[1,192,384]{2,1,0:T(8,128)(2,1)S(1)}, u32[]{:S(2)}) copy-start(bf16[1,192,384]{2,1,0:T(8,128)(2,1)S(1)} %collective-permute-done.16) | copy-start | bytes 442372
  81.6 6.4 %copy-start.27 = (bf16[1,192,384]{2,1,0:T(8,128)(2,1)}, bf16[1,192,384]{2,1,0:T(8,128)(2,1)S(1)}, u32[]{:S(2)}) copy-start(bf16[1,192,384]{2,1,0:T(8,128)(2,1)S(1)} %collective-permute-done.15) | copy-start | bytes 442372
  88.0 0.8 copy-start.6
  88.8 1.3 collective-permute-start.17
  90.2 4.6 %collective-permute-start.18 = (bf16[8,192]{1,0:T(8,128)(2,1)S(1)}, bf16[8,192]{1,0:T(8,128)(2,1)S(1)}, u32[]{:S(2)}, u32[]{:S(2)}) collective-permute-start(bf16[8,192]{1,0:T(8,128)(2,1)S(1)} %pad_maximum_fusion.10), channel_id=1, source_target_pairs={{0,30},{1,31},{2,0},{3,1},{4,2},{5,3},{6,4},{7,5},{8,6},{9,7},{10,... | collective-permute-start | bytes 9224 | tf_op jit(solution)/shard_map/ppermute | solution.py:12
  94.8 3.8 %collective-permute-start.19 = (bf16[16,192]{1,0:T(8,128)(2,1)S(1)}, bf16[16,192]{1,0:T(8,128)(2,1)S(1)}, u32[]{:S(2)}, u32[]{:S(2)}) collective-permute-start(bf16[16,192]{1,0:T(8,128)(2,1)S(1)} %pad_maximum_fusion.8), channel_id=1, source_target_pairs={{0,28},{1,29},{2,30},{3,31},{4,0},{5,1},{6,2},{7,3},{8,4},{9,5},{1... | collective-permute-start | bytes 18440 | tf_op jit(solution)/shard_map/ppermute | solution.py:12
  98.6 3.8 %collective-permute-start.20 = (bf16[32,192]{1,0:T(8,128)(2,1)S(1)}, bf16[32,192]{1,0:T(8,128)(2,1)S(1)}, u32[]{:S(2)}, u32[]{:S(2)}) collective-permute-start(bf16[32,192]{1,0:T(8,128)(2,1)S(1)} %pad_maximum_fusion.6), channel_id=1, source_target_pairs={{0,24},{1,25},{2,26},{3,27},{4,28},{5,29},{6,30},{7,31},{8,0},{9,1... | collective-permute-start | bytes 36872 | tf_op jit(solution)/shard_map/ppermute | solution.py:12
  102.4 7.2 %copy-start.33 = (f32[4,128]{1,0:T(4,128)S(1)}, f32[4,128]{1,0:T(4,128)}, u32[]{:S(2)}) copy-start(f32[4,128]{1,0:T(4,128)} %param.13) | copy-start | bytes 6148
  102.4 7.2 %collective-permute-start.21 = (bf16[64,192]{1,0:T(8,128)(2,1)S(1)}, bf16[64,192]{1,0:T(8,128)(2,1)S(1)}, u32[]{:S(2)}, u32[]{:S(2)}) collective-permute-start(bf16[64,192]{1,0:T(8,128)(2,1)S(1)} %concatenate.49), channel_id=1, source_target_pairs={{0,16},{1,17},{2,18},{3,19},{4,20},{5,21},{6,22},{7,23},{8,24},{9,... | collective-permute-start | bytes 73736 | tf_op jit(solution)/shard_map/ppermute | solution.py:12
  109.6 2.1 %copy-start.36 = (f32[4]{0:T(128)S(1)}, f32[4]{0:T(128)}, u32[]{:S(2)}) copy-start(f32[4]{0:T(128)} %multiply_bitcast_fusion) | copy-start | bytes 52
  114.6 17.0 %copy-start.38 = (bf16[1,1,4,384,384]{4,3,2,1,0:T(8,128)(2,1)S(1)}, bf16[1,1,4,384,384]{4,3,2,1,0:T(8,128)(2,1)}, u32[]{:S(2)}) copy-start(bf16[1,1,4,384,384]{4,3,2,1,0:T(8,128)(2,1)} %param.10) | copy-start | bytes 3538948
  114.7 10.9 %collective-permute-start.22 = (bf16[1,192,384]{2,1,0:T(8,128)(2,1)S(1)}, bf16[1,192,384]{2,1,0:T(8,128)(2,1)S(1)}, u32[]{:S(2)}, u32[]{:S(2)}) collective-permute-start(bf16[1,192,384]{2,1,0:T(8,128)(2,1)S(1)} %get-tuple-element.12), channel_id=1, source_target_pairs={{0,2},{2,4},{4,6},{6,8},{8,10},{10,12},{12,14},{14,16},{16,18},{18... | collective-permute-start | bytes 442376 | tf_op jit(solution)/shard_map/ppermute | solution.py:24
  119.3 6.3 %collective-permute-start.25 = (bf16[1,192,384]{2,1,0:T(8,128)(2,1)S(1)}, bf16[1,192,384]{2,1,0:T(8,128)(2,1)S(1)}, u32[]{:S(2)}, u32[]{:S(2)}) collective-permute-start(bf16[1,192,384]{2,1,0:T(8,128)(2,1)S(1)} %get-tuple-element.13), channel_id=1, source_target_pairs={{1,0},{3,2},{5,4},{7,6},{9,8},{11,10},{13,12},{15,14},{17,16},{19,... | collective-permute-start | bytes 442376 | tf_op jit(solution)/shard_map/ppermute | solution.py:27
  120.6 5.0 %collective-permute-start.24 = (bf16[1,192,384]{2,1,0:T(8,128)(2,1)S(1)}, bf16[1,192,384]{2,1,0:T(8,128)(2,1)S(1)}, u32[]{:S(2)}, u32[]{:S(2)}) collective-permute-start(bf16[1,192,384]{2,1,0:T(8,128)(2,1)S(1)} %get-tuple-element.14), channel_id=1, source_target_pairs={{0,1},{2,3},{4,5},{6,7},{8,9},{10,11},{12,13},{14,15},{16,17},{18,... | collective-permute-start | bytes 442376 | tf_op jit(solution)/shard_map/ppermute | solution.py:24
  123.7 7.9 %collective-permute-start.23 = (bf16[1,192,384]{2,1,0:T(8,128)(2,1)S(1)}, bf16[1,192,384]{2,1,0:T(8,128)(2,1)S(1)}, u32[]{:S(2)}, u32[]{:S(2)}) collective-permute-start(bf16[1,192,384]{2,1,0:T(8,128)(2,1)S(1)} %get-tuple-element.15), channel_id=1, source_target_pairs={{2,0},{4,2},{6,4},{8,6},{10,8},{12,10},{14,12},{16,14},{18,16},{20... | collective-permute-start | bytes 442376 | tf_op jit(solution)/shard_map/ppermute | solution.py:27
  131.6 11.0 %copy-start.9 = (bf16[1,192,384]{2,1,0:T(8,128)(2,1)S(1)}, bf16[1,192,384]{2,1,0:T(8,128)(2,1)}, u32[]{:S(2)}) copy-start(bf16[1,192,384]{2,1,0:T(8,128)(2,1)} %copy-done.7) | copy-start | bytes 442372
  131.6 11.0 %copy-start.12 = (bf16[1,192,384]{2,1,0:T(8,128)(2,1)S(1)}, bf16[1,192,384]{2,1,0:T(8,128)(2,1)}, u32[]{:S(2)}) copy-start(bf16[1,192,384]{2,1,0:T(8,128)(2,1)} %copy-done.10) | copy-start | bytes 442372
  131.6 11.0 %copy-start.15 = (bf16[1,192,384]{2,1,0:T(8,128)(2,1)S(1)}, bf16[1,192,384]{2,1,0:T(8,128)(2,1)}, u32[]{:S(2)}) copy-start(bf16[1,192,384]{2,1,0:T(8,128)(2,1)} %copy-done.13) | copy-start | bytes 442372
  131.6 11.1 %copy-start.18 = (bf16[1,192,384]{2,1,0:T(8,128)(2,1)S(1)}, bf16[1,192,384]{2,1,0:T(8,128)(2,1)}, u32[]{:S(2)}) copy-start(bf16[1,192,384]{2,1,0:T(8,128)(2,1)} %copy-done.16) | copy-start | bytes 442372
  131.6 11.1 %copy-start.24 = (bf16[1,192,384]{2,1,0:T(8,128)(2,1)S(1)}, bf16[1,192,384]{2,1,0:T(8,128)(2,1)}, u32[]{:S(2)}) copy-start(bf16[1,192,384]{2,1,0:T(8,128)(2,1)} %copy-done.23) | copy-start | bytes 442372
  131.6 11.1 %copy-start.26 = (bf16[1,192,384]{2,1,0:T(8,128)(2,1)S(1)}, bf16[1,192,384]{2,1,0:T(8,128)(2,1)}, u32[]{:S(2)}) copy-start(bf16[1,192,384]{2,1,0:T(8,128)(2,1)} %copy-done.25) | copy-start | bytes 442372
  131.6 11.1 %copy-start.28 = (bf16[1,192,384]{2,1,0:T(8,128)(2,1)S(1)}, bf16[1,192,384]{2,1,0:T(8,128)(2,1)}, u32[]{:S(2)}) copy-start(bf16[1,192,384]{2,1,0:T(8,128)(2,1)} %copy-done.27) | copy-start | bytes 442372
  131.7 11.1 %copy-start.30 = (bf16[1,192,384]{2,1,0:T(8,128)(2,1)S(1)}, bf16[1,192,384]{2,1,0:T(8,128)(2,1)}, u32[]{:S(2)}) copy-start(bf16[1,192,384]{2,1,0:T(8,128)(2,1)} %copy-done.29) | copy-start | bytes 442372
  132.2 10.5 %copy-start.3 = (bf16[1,1,4,192,384]{4,3,2,1,0:T(8,128)(2,1)S(1)}, bf16[1,1,4,192,384]{4,3,2,1,0:T(8,128)(2,1)}, u32[]{:S(2)}) copy-start(bf16[1,1,4,192,384]{4,3,2,1,0:T(8,128)(2,1)} %param.9) | copy-start | bytes 1769476
  132.2 10.5 %copy-start.5 = (bf16[4,192,384]{2,1,0:T(8,128)(2,1)S(1)}, bf16[4,192,384]{2,1,0:T(8,128)(2,1)}, u32[]{:S(2)}) copy-start(bf16[4,192,384]{2,1,0:T(8,128)(2,1)} %copy-done.4) | copy-start | bytes 1769476
  132.3 11.0 %collective-permute-start.26 = (bf16[1,192,384]{2,1,0:T(8,128)(2,1)S(1)}, bf16[1,192,384]{2,1,0:T(8,128)(2,1)S(1)}, u32[]{:S(2)}, u32[]{:S(2)}) collective-permute-start(bf16[1,192,384]{2,1,0:T(8,128)(2,1)S(1)} %get-tuple-element.8), channel_id=1, source_target_pairs={{0,2},{2,4},{4,6},{6,8},{8,10},{10,12},{12,14},{14,16},{16,18},{18... | collective-permute-start | bytes 442376 | tf_op jit(solution)/shard_map/ppermute | solution.py:24
  136.0 7.3 %collective-permute-start.29 = (bf16[1,192,384]{2,1,0:T(8,128)(2,1)S(1)}, bf16[1,192,384]{2,1,0:T(8,128)(2,1)S(1)}, u32[]{:S(2)}, u32[]{:S(2)}) collective-permute-start(bf16[1,192,384]{2,1,0:T(8,128)(2,1)S(1)} %get-tuple-element.9), channel_id=1, source_target_pairs={{1,0},{3,2},{5,4},{7,6},{9,8},{11,10},{13,12},{15,14},{17,16},{19,... | collective-permute-start | bytes 442376 | tf_op jit(solution)/shard_map/ppermute | solution.py:27
  137.3 6.0 %collective-permute-start.28 = (bf16[1,192,384]{2,1,0:T(8,128)(2,1)S(1)}, bf16[1,192,384]{2,1,0:T(8,128)(2,1)S(1)}, u32[]{:S(2)}, u32[]{:S(2)}) collective-permute-start(bf16[1,192,384]{2,1,0:T(8,128)(2,1)S(1)} %get-tuple-element.10), channel_id=1, source_target_pairs={{0,1},{2,3},{4,5},{6,7},{8,9},{10,11},{12,13},{14,15},{16,17},{18,... | collective-permute-start | bytes 442376 | tf_op jit(solution)/shard_map/ppermute | solution.py:24
  140.3 7.9 %collective-permute-start.27 = (bf16[1,192,384]{2,1,0:T(8,128)(2,1)S(1)}, bf16[1,192,384]{2,1,0:T(8,128)(2,1)S(1)}, u32[]{:S(2)}, u32[]{:S(2)}) collective-permute-start(bf16[1,192,384]{2,1,0:T(8,128)(2,1)S(1)} %get-tuple-element.11), channel_id=1, source_target_pairs={{2,0},{4,2},{6,4},{8,6},{10,8},{12,10},{14,12},{16,14},{18,16},{20... | collective-permute-start | bytes 442376 | tf_op jit(solution)/shard_map/ppermute | solution.py:27
  (6 other events, 4.1 us)
